TPU v7x, 512 devices: a whole 4x4x16 slice. The times are simulated.
512 devices in a mesh: outer: 16 (over z), inner: 32 (over y, x, core).
Axes of the slice: x: 4, y: 4, z: 16, core: 2. Of those that a mesh axis runs over, the one named last changes fastest.
Arguments:
- field_slab: float32 [512, 128, 4096], P(None, 'inner', 'outer'), may hold values from -48 to 48, as said below
- start_block: float32 [512, 256], replicated, may hold values from -6 to 6
Outputs:
- factor: float32 [512, 256], replicated
- core_fibres: float32 [256, 128, 4096], P('inner', None, 'outer')
Inputs may be any that keep to these rules, and one draw needn't show every extreme that they name: `field_slab`: real values.
All inputs are finite; a program needn't handle non-finite values.
Results may differ from a plain program's by a relative error of at most 0.00016.
Values sent between devices are 32-bit elements; how exact they have to be, the bound alone decides.
No kernel may reach another device: no remote copies, remote signals or barrier semaphores. Data moves between devices by JAX's collectives and lax.ppermute only.
A program may use at most 64 MiB of HBM per device.

v0:
```python
import jax
import jax.numpy as jnp
from jax import lax
from jax.sharding import PartitionSpec as P

ITERS = 2


def product(first_mat, second_mat):
    return jnp.dot(
        first_mat, second_mat, precision=lax.Precision.HIGHEST, preferred_element_type=jnp.float32
    )


def orthonormal(block):
    chol_factor = jnp.linalg.cholesky(product(block.T, block))
    return lax.linalg.triangular_solve(
        chol_factor, block, left_side=False, lower=True, transpose_a=True
    )


def on_device(field_slab, start_block):
    order_rows = field_slab.shape[0]
    local_shape = field_slab.shape
    unfolded = field_slab.reshape(order_rows, local_shape[1] * local_shape[2])
    gram_local = product(unfolded, unfolded.T)
    subspace = orthonormal(start_block)
    gram_total = lax.psum(gram_local, ("outer", "inner"))
    for sweep_index in range(ITERS):
        subspace = orthonormal(product(gram_total, subspace))
    core_block = product(subspace.T, unfolded).reshape(
        subspace.shape[1], local_shape[1], local_shape[2]
    )
    core_fibres = lax.all_to_all(core_block, "inner", split_axis=0, concat_axis=1, tiled=True)
    return (subspace, core_fibres)


def solution(mesh):
    in_specs = (P(None, "inner", "outer"), P())
    out_specs = (P(), P("inner", None, "outer"))
    return jax.shard_map(
        on_device, mesh=mesh, in_specs=in_specs, out_specs=out_specs, check_vma=False
    )
```

profile of v0, /device:TPU:1, one launch (start us, length us, event | category | flops | bytes accessed | tf_op | source)
XLA Modules:
  0.0 663.9 jit_solution(16527323154972641272)
XLA Ops:
  7.2 7.2 %fusion.2 = f32[512,512]{1,0:T(8,128)} fusion(f32[512,4,256]{2,1,0:T(4,128)} %param.5), kind=kOutput, calls=%fused_computation.8 | convolution fusion | flops 3221225472 | bytes 3145728 | tf_op jit(solution)/shard_map/dot_general | solution.py:10
  14.4 1.0 fusion.52
  15.4 0.1 copy.14
  15.7 11.7 %cholesky.172 = f32[128,128]{1,0:T(8,128)S(1)} custom-call(f32[128,128]{1,0:T(8,128)S(1)} %cholesky.270), custom_call_target="Cholesky" | custom-call | tf_op jit(solution)/shard_map/jit(cholesky)/cholesky | solution.py:16
  27.4 9.8 %custom-call.15 = f32[1,128,128]{1,2,0:T(8,128)S(1)} custom-call(f32[1,128,128]{2,1,0:T(8,128)S(1)} %get-tuple-element.72), custom_call_target="InvertDiagBlocksLowerTriangular" | custom-call | tf_op jit(solution)/shard_map/jit(cholesky)/cholesky | solution.py:16
  37.2 0.2 constant_dynamic-update-slice_fusion.5
  37.5 0.3 convolution_subtract_fusion.5
  37.7 12.0 %cholesky.189 = f32[128,128]{1,0:T(8,128)S(1)} custom-call(f32[128,128]{1,0:T(8,128)S(1)} %convolution_subtract_fusion.5), custom_call_target="Cholesky" | custom-call | tf_op jit(solution)/shard_map/jit(cholesky)/cholesky | solution.py:16
  49.7 0.7 compare_reduce_fusion.4
  51.7 3.8 while.6
  51.7 0.6 fusion.79
  52.3 1.3 bitcast_dynamic-update-slice_fusion.6
  53.6 0.6 fusion.79
  54.2 1.3 bitcast_dynamic-update-slice_fusion.6
  55.5 19.7 %custom-call.16 = f32[2,128,128]{1,2,0:T(8,128)S(1)} custom-call(f32[2,128,128]{2,1,0:T(8,128)S(1)} %get-tuple-element.24), custom_call_target="InvertDiagBlocksLowerTriangular" | custom-call | tf_op jit(solution)/shard_map/triangular_solve/custom-call.0 | solution.py:17
  75.2 0.4 fusion.22
  75.6 1.8 copy.21
  77.4 1.9 copy.17
  79.4 0.6 convolution_subtract_fusion.2
  80.0 0.4 fusion.32
  80.4 406.9 %all-reduce.3.cloned.1.call-done = f32[512,512]{1,0:T(8,128)} async-done(((f32[512,512]{1,0:T(8,128)}), f32[512,512]{1,0:T(8,128)}) %all-reduce.3.cloned.1.call-update) | async-done | bytes 1048592 | tf_op jit(solution)/shard_map/psum | solution.py:28
  487.3 2.2 fusion.5
  489.5 1.0 fusion.53
  490.8 11.7 %cholesky.206 = f32[128,128]{1,0:T(8,128)S(1)} custom-call(f32[128,128]{1,0:T(8,128)S(1)} %cholesky.273), custom_call_target="Cholesky" | custom-call | tf_op jit(solution)/shard_map/jit(cholesky)/cholesky | solution.py:16
  502.5 9.8 %custom-call.17 = f32[1,128,128]{1,2,0:T(8,128)S(1)} custom-call(f32[1,128,128]{2,1,0:T(8,128)S(1)} %get-tuple-element.68), custom_call_target="InvertDiagBlocksLowerTriangular" | custom-call | tf_op jit(solution)/shard_map/jit(cholesky)/cholesky | solution.py:16
  512.3 0.2 constant_dynamic-update-slice_fusion.3
  512.6 0.3 convolution_subtract_fusion.4
  512.8 22.6 %cholesky.223 = f32[128,128]{1,0:T(8,128)S(1)} custom-call(f32[128,128]{1,0:T(8,128)S(1)} %convolution_subtract_fusion.4), custom_call_target="Cholesky" | custom-call | tf_op jit(solution)/shard_map/jit(cholesky)/cholesky | solution.py:16
  535.5 0.7 compare_reduce_fusion.2
  536.2 0.6 compare_reduce_fusion.3
  538.2 4.1 while.7
  538.3 0.6 fusion.80
  538.9 1.4 bitcast_dynamic-update-slice_fusion.7
  540.3 0.6 fusion.80
  540.9 1.4 bitcast_dynamic-update-slice_fusion.7
  542.4 19.7 %custom-call.18 = f32[2,128,128]{1,2,0:T(8,128)S(1)} custom-call(f32[2,128,128]{2,1,0:T(8,128)S(1)} %get-tuple-element.25), custom_call_target="InvertDiagBlocksLowerTriangular" | custom-call | tf_op jit(solution)/shard_map/triangular_solve/custom-call.0 | solution.py:17
  562.1 0.4 fusion.17
  562.5 0.6 convolution_subtract_fusion.1
  563.1 0.4 fusion.28
  563.5 1.0 fusion.9
  564.5 1.0 fusion.54
  565.8 11.7 %cholesky.240 = f32[128,128]{1,0:T(8,128)S(1)} custom-call(f32[128,128]{1,0:T(8,128)S(1)} %cholesky.276), custom_call_target="Cholesky" | custom-call | tf_op jit(solution)/shard_map/jit(cholesky)/cholesky | solution.py:16
  577.5 9.8 %custom-call.19 = f32[1,128,128]{1,2,0:T(8,128)S(1)} custom-call(f32[1,128,128]{2,1,0:T(8,128)S(1)} %get-tuple-element.64), custom_call_target="InvertDiagBlocksLowerTriangular" | custom-call | tf_op jit(solution)/shard_map/jit(cholesky)/cholesky | solution.py:16
  587.3 0.2 constant_dynamic-update-slice_fusion
  587.6 0.3 convolution_subtract_fusion.3
  587.8 11.9 %cholesky.257 = f32[128,128]{1,0:T(8,128)S(1)} custom-call(f32[128,128]{1,0:T(8,128)S(1)} %convolution_subtract_fusion.3), custom_call_target="Cholesky" | custom-call | tf_op jit(solution)/shard_map/jit(cholesky)/cholesky | solution.py:16
  599.8 0.7 compare_reduce_fusion
  600.5 0.6 compare_reduce_fusion.1
  602.5 4.1 while.8
  602.5 0.6 fusion.81
  603.1 1.4 bitcast_dynamic-update-slice_fusion.8
  604.6 0.6 fusion.81
  605.2 1.4 bitcast_dynamic-update-slice_fusion.8
  606.6 19.7 %custom-call.20 = f32[2,128,128]{1,2,0:T(8,128)S(1)} custom-call(f32[2,128,128]{2,1,0:T(8,128)S(1)} %get-tuple-element.26), custom_call_target="InvertDiagBlocksLowerTriangular" | custom-call | tf_op jit(solution)/shard_map/triangular_solve/custom-call.0 | solution.py:17
  626.3 0.4 fusion.15
  626.7 0.6 convolution_subtract_fusion
  627.3 0.4 fusion.24
  627.8 1.9 fusion.13
  629.7 1.6 copy.18
  631.3 6.6 %all-to-all-start = ((f32[256,4,256]{2,1,0:T(4,128)}), f32[256,4,256]{2,1,0:T(4,128)S(1)}, u32[]{:S(2)}, u32[]{:S(2)}) async-start(f32[256,4,256]{2,1,0:T(4,128)} %copy.18), calls=%async_computation | async-start | bytes 2097152 | tf_op jit(solution)/shard_map/all_to_all | solution.py:34
  638.0 1.0 copy.20
  639.0 16.1 %all-to-all-done = f32[256,4,256]{2,1,0:T(4,128)S(1)} async-done(((f32[256,4,256]{2,1,0:T(4,128)}), f32[256,4,256]{2,1,0:T(4,128)S(1)}, u32[]{:S(2)}, u32[]{:S(2)}) %all-to-all-start) | async-done | bytes 1048608 | tf_op jit(solution)/shard_map/all_to_all | solution.py:34
  655.2 0.2 copy.19
  655.4 1.3 all_to_all.16
  (40 shorter events, 1.0 us)
Async XLA Ops:
  7.2 7.2 %copy-start = (f32[512,256]{1,0:T(8,128)S(1)}, f32[512,256]{1,0:T(8,128)}, u32[]{:S(2)}) copy-start(f32[512,256]{1,0:T(8,128)} %param.6) | copy-start | bytes 1572868
  7.2 480.1 %all-reduce.3.cloned.1.call-start = ((), (), s32[]{:S(2)}) async-start(), calls=%async_computation.1 | async-start | bytes 2097152 | tf_op jit(solution)/shard_map/psum | solution.py:28
  15.6 60.0 %copy-start.2 = (f32[512,4,256]{2,1,0:T(4,128)S(1)}, f32[512,4,256]{2,1,0:T(4,128)}, u32[]{:S(2)}) copy-start(f32[512,4,256]{2,1,0:T(4,128)} %param.5) | copy-start | bytes 6291460
  562.0 1.4 copy-start.1
  631.3 23.8 %all-to-all-start = ((f32[256,4,256]{2,1,0:T(4,128)}), f32[256,4,256]{2,1,0:T(4,128)S(1)}, u32[]{:S(2)}, u32[]{:S(2)}) async-start(f32[256,4,256]{2,1,0:T(4,128)} %copy.18), calls=%async_computation | async-start | bytes 2097152 | tf_op jit(solution)/shard_map/all_to_all | solution.py:34
Sparse Core Ops, SparseCore 0:
  14.5 472.7 all-reduce.2
where the time goes:
time: 673 us; the launch traced here: 664 us
  waiting for transfers between devices  423 us (63%)
  other arithmetic  174 us (26%)
  matrix products  21.1 us (3%)
  local copies, waits for them, and re-layouts  20.3 us (3%)
  between operations  18.7 us (3%)
    psum x1, waiting for transfers between devices, on_device(): gram_total = lax.psum(gram_local, ('outer', 'inner'))  407 us
    another operation x20, other arithmetic, orthonormal(): chol_factor = jnp.linalg.cholesky(product(block.T, block))  115 us
    another operation x8, other arithmetic, orthonormal(): lax.linalg.triangular_solve(chol_factor, block, left_side=False, lower=Tr...  59.2 us
    all_to_all x1, waiting for transfers between devices, on_device(): lax.all_to_all(core_block, 'inner', split_axis=0, concat_axis=1, tiled=True)  16.1 us
    dot_general x7, matrix products, product(): jnp.dot(first_mat, second_mat, precision=lax.Precision.HIGHEST, preferred...  15.4 us
  transfers between devices with their start and end apart: 2, of which 2 were waited for; matrix products, arithmetic and copies ran while one was open for 10% of the time, Pallas kernels for 0%

commit v1 on v0

--- a/solution.py
+++ b/solution.py
@@ -19,13 +19,31 @@
     )
 
 
-def on_device(field_slab, start_block):
+def scatter_sum(block, axis_name, parts):
+    pieces = block.reshape(parts, block.shape[0] // parts, *block.shape[1:])
+    return lax.all_to_all(pieces, axis_name, 0, 0, tiled=True).sum(0)
+
+
+def gather_rows(block, axis_name, parts):
+    copies = jnp.broadcast_to(block[None], (parts,) + block.shape)
+    gathered = lax.all_to_all(copies, axis_name, 0, 0, tiled=True)
+    return gathered.reshape(parts * block.shape[0], *block.shape[1:])
+
+
+def sum_everywhere(block, sizes):
+    partial = scatter_sum(block, "inner", sizes["inner"])
+    partial = scatter_sum(partial, "outer", sizes["outer"])
+    partial = gather_rows(partial, "outer", sizes["outer"])
+    return gather_rows(partial, "inner", sizes["inner"])
+
+
+def on_device(field_slab, start_block, sizes):
     order_rows = field_slab.shape[0]
     local_shape = field_slab.shape
     unfolded = field_slab.reshape(order_rows, local_shape[1] * local_shape[2])
     gram_local = product(unfolded, unfolded.T)
     subspace = orthonormal(start_block)
-    gram_total = lax.psum(gram_local, ("outer", "inner"))
+    gram_total = sum_everywhere(gram_local, sizes)
     for sweep_index in range(ITERS):
         subspace = orthonormal(product(gram_total, subspace))
     core_block = product(subspace.T, unfolded).reshape(
@@ -36,8 +54,10 @@
 
 
 def solution(mesh):
+    sizes = dict(mesh.shape)
     in_specs = (P(None, "inner", "outer"), P())
     out_specs = (P(), P("inner", None, "outer"))
     return jax.shard_map(
-        on_device, mesh=mesh, in_specs=in_specs, out_specs=out_specs, check_vma=False
+        lambda f, s: on_device(f, s, sizes),
+        mesh=mesh, in_specs=in_specs, out_specs=out_specs, check_vma=False,
     )

time: 673 us -> 320 us (0.48)
  waiting for transfers between devices: 423 us -> 37 us
  starting transfers between devices: 6.68 us -> 44.6 us
  between operations: 18.7 us -> 5.3 us
  local copies, waits for them, and re-layouts: 20.3 us -> 33 us
    psum x1 -> x0, waiting for transfers between devices: 407 us -> none  [on_device(): gram_total = lax.psum(gram_local, ('outer', 'inner'))]
    all_to_all x0 -> x4, starting transfers between devices: none -> 37.3 us  [the longest x2 24.1 us: scatter_sum(): return lax.all_to_all(pieces, axis_name, 0, 0, tiled=True).sum(0)]
    all_to_all x0 -> x4, waiting for transfers between devices: none -> 20.9 us  [the longest x2 11.4 us: gather_rows(): gathered = lax.all_to_all(copies, axis_name, 0, 0, tiled=True)]
    another operation x20, other arithmetic: 115 us -> 104 us  [orthonormal(): chol_factor = jnp.linalg.cholesky(product(block.T, block))]
  transfers between devices with their start and end apart: 2 -> 5, of which waited for: 2 -> 3; matrix products, arithmetic and copies ran while one was open for 10% -> 22% of each run, Pallas kernels for 0% -> 0%
where the time goes in v1:
time: 320 us; the launch traced here: 314 us
  other arithmetic  168 us (52%)
  starting transfers between devices  44.6 us (14%)
  waiting for transfers between devices  37 us (12%)
  local copies, waits for them, and re-layouts  33 us (10%)
  matrix products  26.6 us (8%)
  between operations  5.3 us (2%)
    another operation x20, other arithmetic, orthonormal(): chol_factor = jnp.linalg.cholesky(product(block.T, block))  104 us
    another operation x8, other arithmetic, orthonormal(): lax.linalg.triangular_solve(chol_factor, block, left_side=False, lower=Tr...  61.7 us
    all_to_all x2, starting transfers between devices, scatter_sum(): return lax.all_to_all(pieces, axis_name, 0, 0, tiled=True).sum(0)  24.1 us
    all_to_all x1, waiting for transfers between devices, on_device(): lax.all_to_all(core_block, 'inner', split_axis=0, concat_axis=1, tiled=True)  16.1 us
    dot_general x7, matrix products, product(): jnp.dot(first_mat, second_mat, precision=lax.Precision.HIGHEST, preferred...  14.7 us
    all_to_all x2, starting transfers between devices, gather_rows(): gathered = lax.all_to_all(copies, axis_name, 0, 0, tiled=True)  13.2 us
    another operation x22, local copies, waits for them, and re-layouts, orthonormal(): lax.linalg.triangular_solve(chol_factor, block, left_side=False, lower=Tr...  12 us
    all_to_all x2, waiting for transfers between devices, gather_rows(): gathered = lax.all_to_all(copies, axis_name, 0, 0, tiled=True)  11.4 us
  transfers between devices with their start and end apart: 5, of which 3 were waited for; matrix products, arithmetic and copies ran while one was open for 22% of the time, Pallas kernels for 0%

profile of v1, /device:TPU:1, one launch (start us, length us, event | category | flops | bytes accessed | tf_op | source)
XLA Modules:
  0.0 314.5 jit_solution(10493312807269299587)
XLA Ops:
  0.6 3.5 %dot_general.27 = f32[32,16,1024]{2,1,0:T(8,128)} reshape(f32[512,4,256]{2,1,0:T(4,128)} %param.5) | data formatting | bytes 4194304 | tf_op jit(solution)/shard_map/dot_general | solution.py:10
  4.1 2.1 reshape.79
  6.2 6.7 %fusion.47 = f32[32,16,512]{2,1,0:T(8,128)} fusion(f32[32,16,1024]{2,1,0:T(8,128)} %dot_general.27, f32[512,1024,1]{1,0,2:T(8,128)} %reshape.79), kind=kOutput, calls=%fused_computation.94 | convolution fusion | flops 3221225472 | bytes 5242880 | tf_op jit(solution)/shard_map/dot_general | solution.py:10
  12.9 11.6 %all-to-all-start = ((f32[32,16,512]{2,1,0:T(8,128)}), f32[32,16,512]{2,1,0:T(8,128)}, u32[]{:S(2)}, u32[]{:S(2)}) async-start(f32[32,16,512]{2,1,0:T(8,128)} %fusion.47), calls=%async_computation | async-start | bytes 2097152 | tf_op jit(solution)/shard_map/all_to_all | solution.py:24
  24.6 1.0 fusion.48
  25.8 11.7 %cholesky.172 = f32[128,128]{1,0:T(8,128)S(1)} custom-call(f32[128,128]{1,0:T(8,128)S(1)} %cholesky.270), custom_call_target="Cholesky" | custom-call | tf_op jit(solution)/shard_map/jit(cholesky)/cholesky | solution.py:16
  37.6 9.8 %custom-call.15 = f32[1,128,128]{1,2,0:T(8,128)S(1)} custom-call(f32[1,128,128]{2,1,0:T(8,128)S(1)} %get-tuple-element.72), custom_call_target="InvertDiagBlocksLowerTriangular" | custom-call | tf_op jit(solution)/shard_map/jit(cholesky)/cholesky | solution.py:16
  47.9 11.7 %cholesky.189 = f32[128,128]{1,0:T(8,128)S(1)} custom-call(f32[128,128]{1,0:T(8,128)S(1)} %convolution_subtract_fusion.5), custom_call_target="Cholesky" | custom-call | tf_op jit(solution)/shard_map/jit(cholesky)/cholesky | solution.py:16
  59.6 1.3 reduce_sum.18
  60.9 0.6 reshape.42
  61.5 12.4 %all-to-all-start.1 = ((f32[16,1,512]{2,1,0:T(1,128)}), f32[16,1,512]{2,1,0:T(1,128)S(1)}, u32[]{:S(2)}, u32[]{:S(2)}) async-start(f32[16,1,512]{2,1,0:T(1,128)} %reshape.42), calls=%async_computation.1 | async-start | bytes 65536 | tf_op jit(solution)/shard_map/all_to_all | solution.py:24
  74.0 0.7 compare_reduce_fusion.4
  76.1 9.5 %all-to-all-done.1 = f32[16,1,512]{2,1,0:T(1,128)S(1)} async-done(((f32[16,1,512]{2,1,0:T(1,128)}), f32[16,1,512]{2,1,0:T(1,128)S(1)}, u32[]{:S(2)}, u32[]{:S(2)}) %all-to-all-start.1) | async-done | bytes 32800 | tf_op jit(solution)/shard_map/all_to_all | solution.py:24
  86.2 3.5 %all-to-all-start.2 = ((f32[16,1,512]{2,1,0:T(1,128)}), f32[16,1,512]{2,1,0:T(1,128)S(1)}, u32[]{:S(2)}, u32[]{:S(2)}) async-start(f32[16,1,512]{2,1,0:T(1,128)} %broadcast_in_dim.7), calls=%async_computation.2 | async-start | bytes 65536 | tf_op jit(solution)/shard_map/all_to_all | solution.py:29
  89.8 11.4 %all-to-all-done.2 = f32[16,1,512]{2,1,0:T(1,128)S(1)} async-done(((f32[16,1,512]{2,1,0:T(1,128)}), f32[16,1,512]{2,1,0:T(1,128)S(1)}, u32[]{:S(2)}, u32[]{:S(2)}) %all-to-all-start.2) | async-done | bytes 32800 | tf_op jit(solution)/shard_map/all_to_all | solution.py:29
  101.2 1.1 broadcast_in_dim.16
  102.3 9.7 %all-to-all-start.3 = ((f32[32,16,512]{2,1,0:T(8,128)}), f32[32,16,512]{2,1,0:T(8,128)S(1)}, u32[]{:S(2)}, u32[]{:S(2)}) async-start(f32[32,16,512]{2,1,0:T(8,128)} %broadcast_in_dim.16), calls=%async_computation.3 | async-start | bytes 2097152 | tf_op jit(solution)/shard_map/all_to_all | solution.py:29
  112.1 3.8 %while.6 = (s32[]{:T(128)}, f32[256,256]{1,0:T(8,128)S(1)}, s32[2,2]{1,0:T(2,128)S(1)}, f32[2,128,128]{2,1,0:T(8,128)S(1)}, s32[]{:T(128)}) while((s32[]{:T(128)}, f32[256,256]{1,0:T(8,128)S(1)}, s32[2,2]{1,0:T(2,128)S(1)}, f32[2,128,128]{2,1,0:T(8,128)S(1)}, s32[]{:T(128)}) %tuple.66), condition=%wide.while_cond, body=%wide.while_body.sunk | while | flops 2 | bytes 131189 | solution.py:17
  112.7 1.3 bitcast_dynamic-update-slice_fusion.6
  114.6 1.3 bitcast_dynamic-update-slice_fusion.6
  116.6 20.5 %custom-call.16 = f32[2,128,128]{1,2,0:T(8,128)S(1)} custom-call(f32[2,128,128]{2,1,0:T(8,128)} %copy-done.8), custom_call_target="InvertDiagBlocksLowerTriangular" | custom-call | tf_op jit(solution)/shard_map/triangular_solve/custom-call.0 | solution.py:17
  137.0 1.8 copy.18
  138.9 2.3 copy.13
  141.2 1.4 fusion.17
  142.6 1.6 convolution_subtract_fusion.2
  144.2 1.1 fusion.27
  145.3 2.0 fusion
  147.3 0.8 copy-done.3
  148.1 1.0 fusion.49
  149.1 0.8 copy.11
  149.9 1.0 fusion.15
  150.9 0.7 copy-done.7
  151.6 11.7 %cholesky.206 = f32[128,128]{1,0:T(8,128)S(1)} custom-call(f32[128,128]{1,0:T(8,128)S(1)} %cholesky.273), custom_call_target="Cholesky" | custom-call | tf_op jit(solution)/shard_map/jit(cholesky)/cholesky | solution.py:16
  163.4 9.8 %custom-call.17 = f32[1,128,128]{1,2,0:T(8,128)S(1)} custom-call(f32[1,128,128]{2,1,0:T(8,128)S(1)} %get-tuple-element.68), custom_call_target="InvertDiagBlocksLowerTriangular" | custom-call | tf_op jit(solution)/shard_map/jit(cholesky)/cholesky | solution.py:16
  173.2 1.0 constant_dynamic-update-slice_fusion.3
  174.3 1.1 convolution_subtract_fusion.4
  175.4 11.9 %cholesky.223 = f32[128,128]{1,0:T(8,128)S(1)} custom-call(f32[128,128]{1,0:T(8,128)S(1)} %convolution_subtract_fusion.4), custom_call_target="Cholesky" | custom-call | tf_op jit(solution)/shard_map/jit(cholesky)/cholesky | solution.py:16
  187.2 0.7 compare_reduce_fusion.3
  189.9 1.0 select_select_fusion.1
  190.9 4.1 %while.7 = (s32[]{:T(128)}, f32[256,256]{1,0:T(8,128)S(1)}, s32[2,2]{1,0:T(2,128)S(1)}, f32[2,128,128]{2,1,0:T(8,128)S(1)}, s32[]{:T(128)}) while((s32[]{:T(128)}, f32[256,256]{1,0:T(8,128)S(1)}, s32[2,2]{1,0:T(2,128)S(1)}, f32[2,128,128]{2,1,0:T(8,128)S(1)}, s32[]{:T(128)}) %tuple.75), condition=%wide.while_cond.clone, body=%wide.while_body.clone.sunk | while | flops 2 | bytes 131189 | solution.py:17
  191.5 1.4 bitcast_dynamic-update-slice_fusion.7
  193.6 1.4 bitcast_dynamic-update-slice_fusion.7
  195.0 0.6 copy-done.9
  195.7 20.5 %custom-call.18 = f32[2,128,128]{1,2,0:T(8,128)S(1)} custom-call(f32[2,128,128]{2,1,0:T(8,128)} %copy-done.9), custom_call_target="InvertDiagBlocksLowerTriangular" | custom-call | tf_op jit(solution)/shard_map/triangular_solve/custom-call.0 | solution.py:17
  216.2 1.4 fusion.12
  217.5 1.5 convolution_subtract_fusion.1
  219.5 1.0 fusion.4
  220.6 0.8 copy-done.1
  221.3 1.0 fusion.50
  222.6 11.7 %cholesky.240 = f32[128,128]{1,0:T(8,128)S(1)} custom-call(f32[128,128]{1,0:T(8,128)S(1)} %cholesky.276), custom_call_target="Cholesky" | custom-call | tf_op jit(solution)/shard_map/jit(cholesky)/cholesky | solution.py:16
  234.4 9.8 %custom-call.19 = f32[1,128,128]{1,2,0:T(8,128)S(1)} custom-call(f32[1,128,128]{2,1,0:T(8,128)S(1)} %get-tuple-element.64), custom_call_target="InvertDiagBlocksLowerTriangular" | custom-call | tf_op jit(solution)/shard_map/jit(cholesky)/cholesky | solution.py:16
  244.6 11.9 %cholesky.257 = f32[128,128]{1,0:T(8,128)S(1)} custom-call(f32[128,128]{1,0:T(8,128)S(1)} %convolution_subtract_fusion.3), custom_call_target="Cholesky" | custom-call | tf_op jit(solution)/shard_map/jit(cholesky)/cholesky | solution.py:16
  256.6 0.6 compare_reduce_fusion.1
  257.2 0.7 compare_reduce_fusion
  259.3 4.1 %while.8 = (s32[]{:T(128)}, f32[256,256]{1,0:T(8,128)S(1)}, s32[2,2]{1,0:T(2,128)S(1)}, f32[2,128,128]{2,1,0:T(8,128)S(1)}, s32[]{:T(128)}) while((s32[]{:T(128)}, f32[256,256]{1,0:T(8,128)S(1)}, s32[2,2]{1,0:T(2,128)S(1)}, f32[2,128,128]{2,1,0:T(8,128)S(1)}, s32[]{:T(128)}) %tuple.76), condition=%wide.while_cond.clone.1, body=%wide.while_body.clone.1.sunk | while | flops 2 | bytes 131189 | solution.py:17
  260.0 1.4 bitcast_dynamic-update-slice_fusion.8
  262.0 1.4 bitcast_dynamic-update-slice_fusion.8
  263.5 19.7 %custom-call.20 = f32[2,128,128]{1,2,0:T(8,128)S(1)} custom-call(f32[2,128,128]{2,1,0:T(8,128)S(1)} %get-tuple-element.26), custom_call_target="InvertDiagBlocksLowerTriangular" | custom-call | tf_op jit(solution)/shard_map/triangular_solve/custom-call.0 | solution.py:17
  284.6 1.9 fusion.8
  286.5 1.6 copy.14
  288.2 7.4 %all-to-all-start.4 = ((f32[256,4,256]{2,1,0:T(4,128)}), f32[256,4,256]{2,1,0:T(4,128)S(1)}, u32[]{:S(2)}, u32[]{:S(2)}) async-start(f32[256,4,256]{2,1,0:T(4,128)} %copy.14), calls=%async_computation.4 | async-start | bytes 2097152 | tf_op jit(solution)/shard_map/all_to_all | solution.py:52
  295.6 1.0 copy.16
  296.6 16.1 %all-to-all-done.4 = f32[256,4,256]{2,1,0:T(4,128)S(1)} async-done(((f32[256,4,256]{2,1,0:T(4,128)}), f32[256,4,256]{2,1,0:T(4,128)S(1)}, u32[]{:S(2)}, u32[]{:S(2)}) %all-to-all-start.4) | async-done | bytes 1048608 | tf_op jit(solution)/shard_map/all_to_all | solution.py:52
  312.9 1.3 all_to_all.32
  (67 shorter events, 9.3 us)
Async XLA Ops:
  0.6 3.5 %copy-start = (f32[512,4,256]{2,1,0:T(4,128)S(1)}, f32[512,4,256]{2,1,0:T(4,128)}, u32[]{:S(2)}) copy-start(f32[512,4,256]{2,1,0:T(4,128)} %param.5) | copy-start | bytes 6291460
  12.9 11.6 %copy-start.4 = (f32[512,256]{1,0:T(8,128)S(1)}, f32[512,256]{1,0:T(8,128)}, u32[]{:S(2)}) copy-start(f32[512,256]{1,0:T(8,128)} %param.6) | copy-start | bytes 1572868
  12.9 46.6 %all-to-all-start = ((f32[32,16,512]{2,1,0:T(8,128)}), f32[32,16,512]{2,1,0:T(8,128)}, u32[]{:S(2)}, u32[]{:S(2)}) async-start(f32[32,16,512]{2,1,0:T(8,128)} %fusion.47), calls=%async_computation | async-start | bytes 2097152 | tf_op jit(solution)/shard_map/all_to_all | solution.py:24
  61.5 24.0 %all-to-all-start.1 = ((f32[16,1,512]{2,1,0:T(1,128)}), f32[16,1,512]{2,1,0:T(1,128)S(1)}, u32[]{:S(2)}, u32[]{:S(2)}) async-start(f32[16,1,512]{2,1,0:T(1,128)} %reshape.42), calls=%async_computation.1 | async-start | bytes 65536 | tf_op jit(solution)/shard_map/all_to_all | solution.py:24
  86.2 14.9 %all-to-all-start.2 = ((f32[16,1,512]{2,1,0:T(1,128)}), f32[16,1,512]{2,1,0:T(1,128)S(1)}, u32[]{:S(2)}, u32[]{:S(2)}) async-start(f32[16,1,512]{2,1,0:T(1,128)} %broadcast_in_dim.7), calls=%async_computation.2 | async-start | bytes 65536 | tf_op jit(solution)/shard_map/all_to_all | solution.py:29
  102.3 43.0 %all-to-all-start.3 = ((f32[32,16,512]{2,1,0:T(8,128)}), f32[32,16,512]{2,1,0:T(8,128)S(1)}, u32[]{:S(2)}, u32[]{:S(2)}) async-start(f32[32,16,512]{2,1,0:T(8,128)} %broadcast_in_dim.16), calls=%async_computation.3 | async-start | bytes 2097152 | tf_op jit(solution)/shard_map/all_to_all | solution.py:29
  115.9 0.6 copy-start.8
  115.9 22.9 %copy-start.5 = (f32[256,256]{1,0:T(8,128)}, f32[256,256]{1,0:T(8,128)S(1)}, u32[]{:S(2)}) copy-start(f32[256,256]{1,0:T(8,128)S(1)} %get-tuple-element.219) | copy-start | bytes 786436
  147.3 0.8 copy-start.3
  150.9 0.7 copy-start.7
  188.0 1.9 copy-start.6
  195.0 0.7 copy-start.9
  220.5 0.8 copy-start.1
  222.4 60.8 %copy-start.2 = (f32[512,256]{1,0:T(8,128)S(1)}, f32[512,256]{1,0:T(8,128)}, u32[]{:S(2)}) copy-start(f32[512,256]{1,0:T(8,128)} %copy-done.1) | copy-start | bytes 1572868
  288.2 24.6 %all-to-all-start.4 = ((f32[256,4,256]{2,1,0:T(4,128)}), f32[256,4,256]{2,1,0:T(4,128)S(1)}, u32[]{:S(2)}, u32[]{:S(2)}) async-start(f32[256,4,256]{2,1,0:T(4,128)} %copy.14), calls=%async_computation.4 | async-start | bytes 2097152 | tf_op jit(solution)/shard_map/all_to_all | solution.py:52

commit v2 on v1

--- a/solution.py
+++ b/solution.py
@@ -1,9 +1,14 @@
 import jax
 import jax.numpy as jnp
 from jax import lax
+from jax.experimental import pallas as pl
+from jax.experimental.pallas import tpu as pltpu
 from jax.sharding import PartitionSpec as P
 
 ITERS = 2
+
+PANEL = 64
+UNROLL = 8
 
 
 def product(first_mat, second_mat):
@@ -12,11 +17,74 @@
     )
 
 
+def mat(first, second):
+    return jnp.dot(first, second, precision=lax.Precision.HIGHEST, preferred_element_type=jnp.float32)
+
+
+def mat_nt(first, second):
+    return lax.dot_general(
+        first, second, (((1,), (1,)), ((), ())),
+        precision=lax.Precision.HIGHEST, preferred_element_type=jnp.float32,
+    )
+
+
+def leaf_inverse_factor(diag_block):
+    size = diag_block.shape[0]
+    sub = lax.broadcasted_iota(jnp.int32, (size, size), 0)
+    lane = lax.broadcasted_iota(jnp.int32, (size, size), 1)
+    sub_col = lax.broadcasted_iota(jnp.int32, (size, 1), 0)
+    lane_row = lax.broadcasted_iota(jnp.int32, (1, size), 1)
+
+    def step(j, carry):
+        rest, inv_rows = carry
+        row = jnp.sum(jnp.where(sub == j, rest, 0.0), axis=0, keepdims=True)
+        col = jnp.sum(jnp.where(lane == j, rest, 0.0), axis=1, keepdims=True)
+        pivot = jnp.sum(jnp.where(lane_row == j, row, 0.0), axis=1, keepdims=True)
+        scale = 1.0 / jnp.sqrt(pivot)
+        factor_col = jnp.where(sub_col >= j, col * scale, 0.0)
+        factor_row = jnp.where(lane_row >= j, row * scale, 0.0)
+        rest = rest - factor_col * factor_row
+        solved = jnp.sum(jnp.where(sub == j, inv_rows, 0.0), axis=0, keepdims=True) * scale
+        below = jnp.where(sub_col > j, factor_col, 0.0)
+        inv_rows = jnp.where(sub == j, solved, inv_rows - below * solved)
+        return rest, inv_rows
+
+    start = jnp.where(sub == lane, 1.0, 0.0).astype(jnp.float32)
+    _, inv_rows = lax.fori_loop(0, size, step, (diag_block, start), unroll=UNROLL)
+    return inv_rows
+
+
+def orth_kernel(gram_ref, block_ref, out_ref, rest_ref, inv_ref):
+    order = gram_ref.shape[0]
+    rest_ref[...] = gram_ref[...]
+    eye_sub = lax.broadcasted_iota(jnp.int32, (order, order), 0)
+    eye_lane = lax.broadcasted_iota(jnp.int32, (order, order), 1)
+    inv_ref[...] = jnp.where(eye_sub == eye_lane, 1.0, 0.0).astype(jnp.float32)
+    rows = lax.broadcasted_iota(jnp.int32, (order, 1), 0)
+    for panel in range(order // PANEL):
+        low = panel * PANEL
+        pick_sub = lax.broadcasted_iota(jnp.int32, (PANEL, order), 0)
+        pick_lane = lax.broadcasted_iota(jnp.int32, (PANEL, order), 1)
+        pick = jnp.where(pick_lane == pick_sub + low, 1.0, 0.0).astype(jnp.float32)
+        cols = mat_nt(rest_ref[...], pick)
+        diag_inv = leaf_inverse_factor(cols[low:low + PANEL, :])
+        factor = jnp.where(rows >= low, mat_nt(cols, diag_inv), 0.0)
+        rest_ref[...] = rest_ref[...] - mat_nt(factor, factor)
+        solved = mat(diag_inv, inv_ref[low:low + PANEL, :])
+        below = jnp.where(rows >= low + PANEL, factor, 0.0)
+        inv_ref[...] = inv_ref[...] - mat(below, solved)
+        inv_ref[low:low + PANEL, :] = solved
+    out_ref[...] = mat_nt(block_ref[...], inv_ref[...])
+
+
 def orthonormal(block):
-    chol_factor = jnp.linalg.cholesky(product(block.T, block))
-    return lax.linalg.triangular_solve(
-        chol_factor, block, left_side=False, lower=True, transpose_a=True
-    )
+    gram = jnp.dot(block.T, block, precision=lax.Precision.HIGHEST, preferred_element_type=jnp.float32)
+    order = block.shape[1]
+    return pl.pallas_call(
+        orth_kernel,
+        out_shape=jax.ShapeDtypeStruct(block.shape, jnp.float32),
+        scratch_shapes=[pltpu.VMEM((order, order), jnp.float32), pltpu.VMEM((order, order), jnp.float32)],
+    )(gram, block)
 
 
 def scatter_sum(block, axis_name, parts):

time: 320 us -> 246 us (0.77); the launches traced: 314 us -> 246 us
  other arithmetic: 168 us -> 0.11 us
  Pallas kernels: 0 us -> 113 us
  blocking collectives: 0 us -> 90.2 us
  starting transfers between devices: 44.6 us -> 6.53 us
  waiting for transfers between devices: 37 us -> 0.01 us
  local copies, waits for them, and re-layouts: 33 us -> 14.2 us
  matrix products: 26.6 us -> 20.7 us
  between operations: 5.3 us -> 0.75 us
    another operation x28 -> x0, other arithmetic: 165 us -> none  [the longest x20 104 us: orthonormal(): chol_factor = jnp.linalg.cholesky(product(block.T, block))]
    pallas_call x0 -> x3, Pallas kernels: none -> 113 us  [orthonormal(): pl.pallas_call(orth_kernel, out_shape=jax.ShapeDtypeStruct(block.shape, j...]
    all_to_all x0 -> x4, blocking collectives: none -> 90.2 us  [the longest x2 51.8 us: scatter_sum(): return lax.all_to_all(pieces, axis_name, 0, 0, tiled=True).sum(0)]
    all_to_all x3 -> x0, starting transfers between devices: 31.4 us -> none  [the longest x2 24.1 us: scatter_sum(): return lax.all_to_all(pieces, axis_name, 0, 0, tiled=True).sum(0)]
    all_to_all x3 -> x0, waiting for transfers between devices: 25.6 us -> none  [the longest x1 16.1 us: on_device(): lax.all_to_all(core_block, 'inner', split_axis=0, concat_axis=1, tiled=True)]
    another operation x28 -> x0, local copies, waits for them, and re-layouts: 12.1 us -> none  [the longest x22 12 us: orthonormal(): lax.linalg.triangular_solve(chol_factor, block, left_side=False, lower=Tr...]
    another operation x15 -> x0, matrix products: 11.9 us -> none  [the longest x9 8.82 us: orthonormal(): lax.linalg.triangular_solve(chol_factor, block, left_side=False, lower=Tr...]
    all_to_all x2 -> x1, waiting for transfers between devices: 11.4 us -> 0.01 us  [gather_rows(): gathered = lax.all_to_all(copies, axis_name, 0, 0, tiled=True)]
  transfers between devices with their start and end apart: 5 -> 1, of which waited for: 3 -> 0; matrix products, arithmetic and copies ran while one was open for 22% -> 3% of each run, Pallas kernels for 0% -> 15%
where the time goes in v2:
time: 246 us
  Pallas kernels  113 us (46%)
  blocking collectives  90.2 us (37%)
  matrix products  20.7 us (8%)
  local copies, waits for them, and re-layouts  14.2 us (6%)
  starting transfers between devices  6.53 us (3%)
    pallas_call x3, Pallas kernels, orthonormal(): pl.pallas_call(orth_kernel, out_shape=jax.ShapeDtypeStruct(block.shape, j...  113 us
    all_to_all x2, blocking collectives, scatter_sum(): return lax.all_to_all(pieces, axis_name, 0, 0, tiled=True).sum(0)  51.8 us
    all_to_all x1, blocking collectives, on_device(): lax.all_to_all(core_block, 'inner', split_axis=0, concat_axis=1, tiled=True)  24.5 us
    dot_general x4, matrix products, product(): jnp.dot(first_mat, second_mat, precision=lax.Precision.HIGHEST, preferred...  14.3 us
    all_to_all x1, blocking collectives, gather_rows(): gathered = lax.all_to_all(copies, axis_name, 0, 0, tiled=True)  14 us
    all_to_all x1, starting transfers between devices, gather_rows(): gathered = lax.all_to_all(copies, axis_name, 0, 0, tiled=True)  6.53 us
    dot_general x3, matrix products, orthonormal(): jnp.dot(block.T, block, precision=lax.Precision.HIGHEST, preferred_elemen...  6.35 us
    dot_general x3, local copies, waits for them, and re-layouts, product(): jnp.dot(first_mat, second_mat, precision=lax.Precision.HIGHEST, preferred...  6.1 us
  transfers between devices with their start and end apart: 1, of which 0 were waited for; matrix products, arithmetic and copies ran while one was open for 3% of the time, Pallas kernels for 15%

profile of v2, /device:TPU:1, one launch (start us, length us, event | category | flops | bytes accessed | tf_op | source)
XLA Modules:
  0.0 245.7 jit_solution(14116949179589016643)
XLA Ops:
  0.6 0.0 copy-start
  0.6 3.5 %dot_general.27 = f32[32,16,1024]{2,1,0:T(8,128)} reshape(f32[512,4,256]{2,1,0:T(4,128)} %param.2) | data formatting | bytes 4194304 | tf_op jit(solution)/shard_map/dot_general | solution.py:15
  4.1 0.0 copy-done
  4.1 2.1 reshape.27
  6.2 5.7 %fusion.2 = f32[32,16,512]{2,1,0:T(8,128)S(1)} fusion(f32[32,16,1024]{2,1,0:T(8,128)} %dot_general.27, f32[512,1024,1]{1,0,2:T(8,128)} %reshape.27), kind=kOutput, calls=%fused_computation.3 | convolution fusion | flops 3221225472 | bytes 5242880 | tf_op jit(solution)/shard_map/dot_general | solution.py:15
  12.0 26.8 %all_to_all.38 = f32[32,16,512]{2,1,0:T(8,128)S(1)} all-to-all(f32[32,16,512]{2,1,0:T(8,128)S(1)} %fusion.2), channel_id=1, replica_groups=mesh['outer'=16,'inner'=32] {'inner'}, dimensions={0} | all-to-all | bytes 2097152 | tf_op jit(solution)/shard_map/all_to_all | solution.py:92
  38.8 0.1 reduce_sum.18
  38.9 24.9 %all_to_all.39 = f32[16,1,512]{2,1,0:T(1,128)S(1)} all-to-all(f32[16,1,512]{2,1,0:T(1,128)S(1)} %reshape.25), channel_id=1, replica_groups=mesh['outer'=16,'inner'=32] {'outer'}, dimensions={0} | all-to-all | bytes 65536 | tf_op jit(solution)/shard_map/all_to_all | solution.py:92
  63.9 14.0 %all_to_all.40 = f32[16,1,512]{2,1,0:T(1,128)S(1)} all-to-all(f32[16,1,512]{2,1,0:T(1,128)S(1)} %broadcast_in_dim.6), channel_id=1, replica_groups=mesh['outer'=16,'inner'=32] {'outer'}, dimensions={0} | all-to-all | bytes 65536 | tf_op jit(solution)/shard_map/all_to_all | solution.py:97
  77.9 1.1 broadcast_in_dim.15
  79.0 6.5 %all-to-all-start.3 = ((f32[32,16,512]{2,1,0:T(8,128)}), f32[32,16,512]{2,1,0:T(8,128)S(1)}, u32[]{:S(2)}, u32[]{:S(2)}) async-start(f32[32,16,512]{2,1,0:T(8,128)} %broadcast_in_dim.15), calls=%async_computation.3 | async-start | bytes 2097152 | tf_op jit(solution)/shard_map/all_to_all | solution.py:97
  85.5 2.9 %fusion.3.gram_ref = f32[256,256]{1,0:T(8,128)} fusion(f32[512,256]{1,0:T(8,128)} %block_ref.1), kind=kOutput, calls=%fused_computation.4 | convolution fusion | flops 402653184 | bytes 786432 | tf_op jit(solution)/shard_map/dot_general | solution.py:81
  88.4 37.6 %shard_map.41 = f32[512,256]{1,0:T(8,128)} custom-call(f32[256,256]{1,0:T(8,128)} %fusion.3.gram_ref, f32[512,256]{1,0:T(8,128)} %block_ref.1), custom_call_target="tpu_custom_call" | custom-call | tf_op jit(solution)/shard_map/pallas_call | solution.py:83
  126.0 1.8 copy.14
  127.8 1.9 copy.7
  129.8 0.0 all-to-all-done.3
  129.8 2.0 fusion.4.block_ref
  131.8 0.0 copy-start.2
  131.8 0.8 copy-done.2
  132.6 1.7 fusion.5.gram_ref
  134.3 37.8 %shard_map.42 = f32[512,256]{1,0:T(8,128)} custom-call(f32[256,256]{1,0:T(8,128)} %fusion.5.gram_ref, f32[512,256]{1,0:T(8,128)} %copy-done.2), custom_call_target="tpu_custom_call" | custom-call | tf_op jit(solution)/shard_map/pallas_call | solution.py:83
  172.1 2.0 fusion.6.block_ref
  174.1 0.0 copy-start.1
  174.2 0.8 copy-done.1
  174.9 1.7 fusion.7.gram_ref
  176.7 37.8 %shard_map.43 = f32[512,256]{1,0:T(8,128)} custom-call(f32[256,256]{1,0:T(8,128)} %fusion.7.gram_ref, f32[512,256]{1,0:T(8,128)} %copy-done.1), custom_call_target="tpu_custom_call" | custom-call | tf_op jit(solution)/shard_map/pallas_call | solution.py:83
  214.5 4.5 %fusion = f32[256,4,256]{2,0,1:T(8,128)S(1)} fusion(f32[4,256,512]{2,1,0:T(8,128)S(1)} %bitcast.31, f32[512,256]{1,0:T(8,128)} %shard_map.43), kind=kOutput, calls=%fused_computation | convolution fusion | flops 1610612736 | bytes 3670016 | tf_op jit(solution)/shard_map/dot_general | solution.py:15
  219.0 0.7 copy.9
  219.7 24.5 %all_to_all.41 = f32[256,4,256]{2,1,0:T(4,128)S(1)} all-to-all(f32[256,4,256]{2,1,0:T(4,128)S(1)} %copy.9), channel_id=1, replica_groups=mesh['outer'=16,'inner'=32] {'inner'}, dimensions={0} | all-to-all | bytes 2097152 | tf_op jit(solution)/shard_map/all_to_all | solution.py:120
  244.2 0.2 copy.10
  244.4 1.3 all_to_all.32
  (4 shorter events, 0.1 us)
Async XLA Ops:
  0.6 3.5 %copy-start = (f32[512,4,256]{2,1,0:T(4,128)S(1)}, f32[512,4,256]{2,1,0:T(4,128)}, u32[]{:S(2)}) copy-start(f32[512,4,256]{2,1,0:T(4,128)} %param.2) | copy-start | bytes 6291460
  79.0 50.8 %all-to-all-start.3 = ((f32[32,16,512]{2,1,0:T(8,128)}), f32[32,16,512]{2,1,0:T(8,128)S(1)}, u32[]{:S(2)}, u32[]{:S(2)}) async-start(f32[32,16,512]{2,1,0:T(8,128)} %broadcast_in_dim.15), calls=%async_computation.3 | async-start | bytes 2097152 | tf_op jit(solution)/shard_map/all_to_all | solution.py:97
  131.8 0.8 copy-start.2
  174.1 0.8 copy-start.1

commit v3 on v2

--- a/solution.py
+++ b/solution.py
@@ -40,7 +40,7 @@
         row = jnp.sum(jnp.where(sub == j, rest, 0.0), axis=0, keepdims=True)
         col = jnp.sum(jnp.where(lane == j, rest, 0.0), axis=1, keepdims=True)
         pivot = jnp.sum(jnp.where(lane_row == j, row, 0.0), axis=1, keepdims=True)
-        scale = 1.0 / jnp.sqrt(pivot)
+        scale = lax.rsqrt(pivot)
         factor_col = jnp.where(sub_col >= j, col * scale, 0.0)
         factor_row = jnp.where(lane_row >= j, row * scale, 0.0)
         rest = rest - factor_col * factor_row
@@ -106,16 +106,17 @@
 
 
 def on_device(field_slab, start_block, sizes):
-    order_rows = field_slab.shape[0]
-    local_shape = field_slab.shape
-    unfolded = field_slab.reshape(order_rows, local_shape[1] * local_shape[2])
-    gram_local = product(unfolded, unfolded.T)
+    gram_local = lax.dot_general(
+        field_slab, field_slab, (((1, 2), (1, 2)), ((), ())),
+        precision=lax.Precision.HIGHEST, preferred_element_type=jnp.float32,
+    )
     subspace = orthonormal(start_block)
     gram_total = sum_everywhere(gram_local, sizes)
     for sweep_index in range(ITERS):
         subspace = orthonormal(product(gram_total, subspace))
-    core_block = product(subspace.T, unfolded).reshape(
-        subspace.shape[1], local_shape[1], local_shape[2]
+    core_block = lax.dot_general(
+        subspace, field_slab, (((0,), (0,)), ((), ())),
+        precision=lax.Precision.HIGHEST, preferred_element_type=jnp.float32,
     )
     core_fibres = lax.all_to_all(core_block, "inner", split_axis=0, concat_axis=1, tiled=True)
     return (subspace, core_fibres)

time: 246 us -> 227 us (0.923)
  local copies, waits for them, and re-layouts: 14.2 us -> 3.37 us
  Pallas kernels: 113 us -> 107 us
    dot_general x4 -> x2, matrix products: 14.3 us -> 4.05 us  [product(): jnp.dot(first_mat, second_mat, precision=lax.Precision.HIGHEST, preferred...]
    dot_general x0 -> x2, matrix products: none -> 9.34 us  [the longest x1 6.16 us: on_device(): lax.dot_general(field_slab, field_slab, (((1, 2), (1, 2)), ((), ())), pre...]
    pallas_call x3, Pallas kernels: 113 us -> 107 us  [orthonormal(): pl.pallas_call(orth_kernel, out_shape=jax.ShapeDtypeStruct(block.shape, j...]
    dot_general x3 -> x1, local copies, waits for them, and re-layouts: 6.1 us -> 0.68 us  [on_device(): lax.dot_general(subspace, field_slab, (((0,), (0,)), ((), ())), precision...]
    unnamed x8 -> x9, local copies, waits for them, and re-layouts: 3.4 us -> 0.03 us
  transfers between devices with their start and end apart: 1 -> 1, of which waited for: 0 -> 0; matrix products, arithmetic and copies ran while one was open for 3% -> 1% of each run, Pallas kernels for 15% -> 16%
where the time goes in v3:
time: 227 us
  Pallas kernels  107 us (47%)
  blocking collectives  90.3 us (40%)
  matrix products  18.5 us (8%)
  starting transfers between devices  6.53 us (3%)
  local copies, waits for them, and re-layouts  3.37 us (1%)
    pallas_call x3, Pallas kernels, orthonormal(): pl.pallas_call(orth_kernel, out_shape=jax.ShapeDtypeStruct(block.shape, j...  107 us
    all_to_all x2, blocking collectives, scatter_sum(): return lax.all_to_all(pieces, axis_name, 0, 0, tiled=True).sum(0)  51.9 us
    all_to_all x1, blocking collectives, on_device(): lax.all_to_all(core_block, 'inner', split_axis=0, concat_axis=1, tiled=True)  24.5 us
    all_to_all x1, blocking collectives, gather_rows(): gathered = lax.all_to_all(copies, axis_name, 0, 0, tiled=True)  14 us
    all_to_all x1, starting transfers between devices, gather_rows(): gathered = lax.all_to_all(copies, axis_name, 0, 0, tiled=True)  6.53 us
    dot_general x1, matrix products, on_device(): lax.dot_general(field_slab, field_slab, (((1, 2), (1, 2)), ((), ())), pre...  6.16 us
    dot_general x3, matrix products, orthonormal(): jnp.dot(block.T, block, precision=lax.Precision.HIGHEST, preferred_elemen...  5.15 us
  transfers between devices with their start and end apart: 1, of which 0 were waited for; matrix products, arithmetic and copies ran while one was open for 1% of the time, Pallas kernels for 16%

profile of v3, /device:TPU:1, one launch (start us, length us, event | category | flops | bytes accessed | tf_op | source)
XLA Modules:
  0.0 226.8 jit_solution(15689481635062306354)
XLA Ops:
  0.6 6.2 %fusion.2 = f32[512,512,1]{1,0,2:T(8,128)S(1)} fusion(f32[512,4,256]{2,1,0:T(4,128)} %param.2), kind=kOutput, calls=%fused_computation.2 | convolution fusion | flops 3221225472 | bytes 3145728 | tf_op jit(solution)/shard_map/dot_general | solution.py:109
  6.8 26.8 %all_to_all.38 = f32[32,16,512]{2,1,0:T(8,128)S(1)} all-to-all(f32[32,16,512]{2,1,0:T(8,128)S(1)} %bitcast.26), channel_id=1, replica_groups=mesh['outer'=16,'inner'=32] {'inner'}, dimensions={0} | all-to-all | bytes 2097152 | tf_op jit(solution)/shard_map/all_to_all | solution.py:92
  33.6 0.0 copy-start.2
  33.6 0.1 reduce_sum.18
  33.7 25.1 %all_to_all.39 = f32[16,1,512]{2,1,0:T(1,128)S(1)} all-to-all(f32[16,1,512]{2,1,0:T(1,128)S(1)} %reshape.20), channel_id=1, replica_groups=mesh['outer'=16,'inner'=32] {'outer'}, dimensions={0} | all-to-all | bytes 65536 | tf_op jit(solution)/shard_map/all_to_all | solution.py:92
  58.9 14.0 %all_to_all.40 = f32[16,1,512]{2,1,0:T(1,128)S(1)} all-to-all(f32[16,1,512]{2,1,0:T(1,128)S(1)} %broadcast_in_dim.6), channel_id=1, replica_groups=mesh['outer'=16,'inner'=32] {'outer'}, dimensions={0} | all-to-all | bytes 65536 | tf_op jit(solution)/shard_map/all_to_all | solution.py:97
  72.8 1.1 broadcast_in_dim.15
  73.9 6.5 %all-to-all-start.3 = ((f32[32,16,512]{2,1,0:T(8,128)}), f32[32,16,512]{2,1,0:T(8,128)S(1)}, u32[]{:S(2)}, u32[]{:S(2)}) async-start(f32[32,16,512]{2,1,0:T(8,128)} %broadcast_in_dim.15), calls=%async_computation.3 | async-start | bytes 2097152 | tf_op jit(solution)/shard_map/all_to_all | solution.py:97
  80.5 0.0 copy-done.2
  80.5 1.7 fusion.5.gram_ref
  82.2 35.6 %shard_map.41 = f32[512,256]{1,0:T(8,128)} custom-call(f32[256,256]{1,0:T(8,128)} %fusion.5.gram_ref, f32[512,256]{1,0:T(8,128)} %block_ref.1), custom_call_target="tpu_custom_call" | custom-call | tf_op jit(solution)/shard_map/pallas_call | solution.py:83
  117.8 0.0 all-to-all-done.3
  117.8 2.0 fusion.6.block_ref
  119.8 0.0 copy-start.1
  119.8 1.7 fusion.7.gram_ref
  121.5 0.0 copy-done.1
  121.5 35.8 %shard_map.42 = f32[512,256]{1,0:T(8,128)} custom-call(f32[256,256]{1,0:T(8,128)} %fusion.7.gram_ref, f32[512,256]{1,0:T(8,128)} %copy-done.1), custom_call_target="tpu_custom_call" | custom-call | tf_op jit(solution)/shard_map/pallas_call | solution.py:83
  157.3 2.0 fusion.8.block_ref
  159.3 0.0 copy-start
  159.3 0.0 copy-start.3
  159.3 1.7 fusion.9.gram_ref
  161.1 0.0 copy-done
  161.1 35.8 %shard_map.43 = f32[512,256]{1,0:T(8,128)} custom-call(f32[256,256]{1,0:T(8,128)} %fusion.9.gram_ref, f32[512,256]{1,0:T(8,128)} %copy-done), custom_call_target="tpu_custom_call" | custom-call | tf_op jit(solution)/shard_map/pallas_call | solution.py:83
  196.9 0.0 copy-done.3
  196.9 3.2 %fusion = f32[256,4,256]{2,0,1:T(8,128)S(1)} fusion(f32[512,4,256]{2,1,0:T(4,128)S(1)} %copy-done.3, f32[512,256]{1,0:T(8,128)} %shard_map.43), kind=kOutput, calls=%fused_computation | convolution fusion | flops 1610612736 | bytes 3670016 | tf_op jit(solution)/shard_map/dot_general | solution.py:117
  200.1 0.7 copy.13
  200.8 24.5 %all_to_all.41 = f32[256,4,256]{2,1,0:T(4,128)S(1)} all-to-all(f32[256,4,256]{2,1,0:T(4,128)S(1)} %copy.13), channel_id=1, replica_groups=mesh['outer'=16,'inner'=32] {'inner'}, dimensions={0} | all-to-all | bytes 2097152 | tf_op jit(solution)/shard_map/all_to_all | solution.py:121
  225.2 0.2 copy.14
  225.4 1.3 all_to_all.32
  (4 shorter events, 0.1 us)
Async XLA Ops:
  33.6 46.8 %copy-start.2 = (f32[512,256]{1,0:T(8,128)S(1)}, f32[512,256]{1,0:T(8,128)}, u32[]{:S(2)}) copy-start(f32[512,256]{1,0:T(8,128)} %block_ref.1) | copy-start | bytes 1572868
  73.9 43.8 %all-to-all-start.3 = ((f32[32,16,512]{2,1,0:T(8,128)}), f32[32,16,512]{2,1,0:T(8,128)S(1)}, u32[]{:S(2)}, u32[]{:S(2)}) async-start(f32[32,16,512]{2,1,0:T(8,128)} %broadcast_in_dim.15), calls=%async_computation.3 | async-start | bytes 2097152 | tf_op jit(solution)/shard_map/all_to_all | solution.py:97
  119.8 1.7 copy-start.1
  159.3 1.7 copy-start
  159.3 37.6 %copy-start.3 = (f32[512,4,256]{2,1,0:T(4,128)S(1)}, f32[512,4,256]{2,1,0:T(4,128)}, u32[]{:S(2)}) copy-start(f32[512,4,256]{2,1,0:T(4,128)} %param.2) | copy-start | bytes 6291460

commit v4 on v3

--- a/solution.py
+++ b/solution.py
@@ -8,7 +8,7 @@
 ITERS = 2
 
 PANEL = 64
-UNROLL = 8
+UNROLL = 1
 
 
 def product(first_mat, second_mat):
@@ -28,53 +28,80 @@
     )
 
 
+GROUP = 8
+
+
 def leaf_inverse_factor(diag_block):
     size = diag_block.shape[0]
-    sub = lax.broadcasted_iota(jnp.int32, (size, size), 0)
-    lane = lax.broadcasted_iota(jnp.int32, (size, size), 1)
+    wide = 2 * size
+    sub = lax.broadcasted_iota(jnp.int32, (size, wide), 0)
+    lane = lax.broadcasted_iota(jnp.int32, (size, wide), 1)
     sub_col = lax.broadcasted_iota(jnp.int32, (size, 1), 0)
-    lane_row = lax.broadcasted_iota(jnp.int32, (1, size), 1)
+    lane_row = lax.broadcasted_iota(jnp.int32, (1, wide), 1)
+    joined = diag_block + jnp.where(lane == sub + size, 1.0, 0.0).astype(jnp.float32)
 
-    def step(j, carry):
-        rest, inv_rows = carry
-        row = jnp.sum(jnp.where(sub == j, rest, 0.0), axis=0, keepdims=True)
-        col = jnp.sum(jnp.where(lane == j, rest, 0.0), axis=1, keepdims=True)
-        pivot = jnp.sum(jnp.where(lane_row == j, row, 0.0), axis=1, keepdims=True)
-        scale = lax.rsqrt(pivot)
-        factor_col = jnp.where(sub_col >= j, col * scale, 0.0)
-        factor_row = jnp.where(lane_row >= j, row * scale, 0.0)
-        rest = rest - factor_col * factor_row
-        solved = jnp.sum(jnp.where(sub == j, inv_rows, 0.0), axis=0, keepdims=True) * scale
-        below = jnp.where(sub_col > j, factor_col, 0.0)
-        inv_rows = jnp.where(sub == j, solved, inv_rows - below * solved)
-        return rest, inv_rows
+    def step(group, carry):
+        rest, solved_rows = carry
+        first = group * GROUP
+        rows = [jnp.sum(jnp.where(sub == first + i, rest, 0.0), axis=0, keepdims=True) for i in range(GROUP)]
+        cols = [jnp.sum(jnp.where(lane == first + i, rest, 0.0), axis=1, keepdims=True) for i in range(GROUP)]
+        pivots = [
+            [jnp.sum(jnp.where(lane_row == first + m, rows[i], 0.0), axis=1, keepdims=True) for m in range(i + 1)]
+            for i in range(GROUP)
+        ]
+        low = [[None] * GROUP for _ in range(GROUP)]
+        scales = []
+        for i in range(GROUP):
+            for r in range(i, GROUP):
+                value = pivots[r][i]
+                for m in range(i):
+                    value = value - low[r][m] * low[i][m]
+                if r == i:
+                    scale = lax.rsqrt(value)
+                    scales.append(scale)
+                    low[i][i] = value * scale
+                else:
+                    low[r][i] = value * scales[i]
+        factor_rows, factor_cols = [], []
+        for i in range(GROUP):
+            row, col = rows[i], cols[i]
+            for m in range(i):
+                row = row - low[i][m] * factor_rows[m]
+                col = col - low[i][m] * factor_cols[m]
+            factor_rows.append(jnp.where(lane_row >= first + i, row * scales[i], 0.0))
+            factor_cols.append(jnp.where(sub_col >= first + i, col * scales[i], 0.0))
+        for i in range(GROUP):
+            rest = rest - factor_cols[i] * factor_rows[i]
+            solved_rows = jnp.where(sub == first + i, factor_rows[i], solved_rows)
+        return rest, solved_rows
 
-    start = jnp.where(sub == lane, 1.0, 0.0).astype(jnp.float32)
-    _, inv_rows = lax.fori_loop(0, size, step, (diag_block, start), unroll=UNROLL)
-    return inv_rows
+    _, solved_rows = lax.fori_loop(0, size // GROUP, step, (joined, jnp.zeros_like(joined)), unroll=UNROLL)
+    swapped = pltpu.roll(solved_rows, size, 1)
+    return jnp.where(lane < size, swapped, 0.0)
 
 
 def orth_kernel(gram_ref, block_ref, out_ref, rest_ref, inv_ref):
     order = gram_ref.shape[0]
+    wide = 2 * PANEL
     rest_ref[...] = gram_ref[...]
-    eye_sub = lax.broadcasted_iota(jnp.int32, (order, order), 0)
-    eye_lane = lax.broadcasted_iota(jnp.int32, (order, order), 1)
+    eye_sub = lax.broadcasted_iota(jnp.int32, inv_ref.shape, 0)
+    eye_lane = lax.broadcasted_iota(jnp.int32, inv_ref.shape, 1)
     inv_ref[...] = jnp.where(eye_sub == eye_lane, 1.0, 0.0).astype(jnp.float32)
     rows = lax.broadcasted_iota(jnp.int32, (order, 1), 0)
+    pick_sub = lax.broadcasted_iota(jnp.int32, (wide, order), 0)
+    pick_lane = lax.broadcasted_iota(jnp.int32, (wide, order), 1)
     for panel in range(order // PANEL):
         low = panel * PANEL
-        pick_sub = lax.broadcasted_iota(jnp.int32, (PANEL, order), 0)
-        pick_lane = lax.broadcasted_iota(jnp.int32, (PANEL, order), 1)
-        pick = jnp.where(pick_lane == pick_sub + low, 1.0, 0.0).astype(jnp.float32)
-        cols = mat_nt(rest_ref[...], pick)
+        pick = jnp.where((pick_lane == pick_sub + low) & (pick_sub < PANEL), 1.0, 0.0)
+        cols = mat_nt(rest_ref[...], pick.astype(jnp.float32))
         diag_inv = leaf_inverse_factor(cols[low:low + PANEL, :])
         factor = jnp.where(rows >= low, mat_nt(cols, diag_inv), 0.0)
         rest_ref[...] = rest_ref[...] - mat_nt(factor, factor)
-        solved = mat(diag_inv, inv_ref[low:low + PANEL, :])
+        solved = mat(diag_inv, inv_ref[low:low + wide, :])
         below = jnp.where(rows >= low + PANEL, factor, 0.0)
-        inv_ref[...] = inv_ref[...] - mat(below, solved)
+        inv_ref[0:order, :] = inv_ref[0:order, :] - mat(below, solved)
         inv_ref[low:low + PANEL, :] = solved
-    out_ref[...] = mat_nt(block_ref[...], inv_ref[...])
+    out_ref[...] = mat_nt(block_ref[...], inv_ref[0:order, :])
 
 
 def orthonormal(block):
@@ -83,7 +110,7 @@
     return pl.pallas_call(
         orth_kernel,
         out_shape=jax.ShapeDtypeStruct(block.shape, jnp.float32),
-        scratch_shapes=[pltpu.VMEM((order, order), jnp.float32), pltpu.VMEM((order, order), jnp.float32)],
+        scratch_shapes=[pltpu.VMEM((order, order), jnp.float32), pltpu.VMEM((order + PANEL, order), jnp.float32)],
     )(gram, block)
 
 

time: 227 us -> 172 us (0.76)
  Pallas kernels: 107 us -> 52 us
    pallas_call x3, Pallas kernels: 107 us -> 52 us  [orthonormal(): pl.pallas_call(orth_kernel, out_shape=jax.ShapeDtypeStruct(block.shape, j...]
  transfers between devices with their start and end apart: 1 -> 1, of which waited for: 0 -> 0; matrix products, arithmetic and copies ran while one was open for 1% -> 1% of each run, Pallas kernels for 16% -> 10%
where the time goes in v4:
time: 172 us
  blocking collectives  90.3 us (52%)
  Pallas kernels  52 us (30%)
  matrix products  18.5 us (11%)
  starting transfers between devices  6.53 us (4%)
  local copies, waits for them, and re-layouts  3.37 us (2%)
    pallas_call x3, Pallas kernels, orthonormal(): pl.pallas_call(orth_kernel, out_shape=jax.ShapeDtypeStruct(block.shape, j...  52 us
    all_to_all x2, blocking collectives, scatter_sum(): return lax.all_to_all(pieces, axis_name, 0, 0, tiled=True).sum(0)  51.9 us
    all_to_all x1, blocking collectives, on_device(): lax.all_to_all(core_block, 'inner', split_axis=0, concat_axis=1, tiled=True)  24.5 us
    all_to_all x1, blocking collectives, gather_rows(): gathered = lax.all_to_all(copies, axis_name, 0, 0, tiled=True)  14 us
    all_to_all x1, starting transfers between devices, gather_rows(): gathered = lax.all_to_all(copies, axis_name, 0, 0, tiled=True)  6.53 us
    dot_general x1, matrix products, on_device(): lax.dot_general(field_slab, field_slab, (((1, 2), (1, 2)), ((), ())), pre...  6.16 us
    dot_general x3, matrix products, orthonormal(): jnp.dot(block.T, block, precision=lax.Precision.HIGHEST, preferred_elemen...  5.15 us
    dot_general x2, matrix products, product(): jnp.dot(first_mat, second_mat, precision=lax.Precision.HIGHEST, preferred...  4.05 us
  transfers between devices with their start and end apart: 1, of which 0 were waited for; matrix products, arithmetic and copies ran while one was open for 1% of the time, Pallas kernels for 10%

profile of v4, /device:TPU:1, one launch (start us, length us, event | category | flops | bytes accessed | tf_op | source)
XLA Modules:
  0.0 171.6 jit_solution(10209539847291058670)
XLA Ops:
  0.6 6.2 %fusion.2 = f32[512,512,1]{1,0,2:T(8,128)S(1)} fusion(f32[512,4,256]{2,1,0:T(4,128)} %param.2), kind=kOutput, calls=%fused_computation.2 | convolution fusion | flops 3221225472 | bytes 3145728 | tf_op jit(solution)/shard_map/dot_general | solution.py:136
  6.8 26.8 %all_to_all.38 = f32[32,16,512]{2,1,0:T(8,128)S(1)} all-to-all(f32[32,16,512]{2,1,0:T(8,128)S(1)} %bitcast.26), channel_id=1, replica_groups=mesh['outer'=16,'inner'=32] {'inner'}, dimensions={0} | all-to-all | bytes 2097152 | tf_op jit(solution)/shard_map/all_to_all | solution.py:119
  33.6 0.0 copy-start.2
  33.6 0.1 reduce_sum.18
  33.7 25.1 %all_to_all.39 = f32[16,1,512]{2,1,0:T(1,128)S(1)} all-to-all(f32[16,1,512]{2,1,0:T(1,128)S(1)} %reshape.20), channel_id=1, replica_groups=mesh['outer'=16,'inner'=32] {'outer'}, dimensions={0} | all-to-all | bytes 65536 | tf_op jit(solution)/shard_map/all_to_all | solution.py:119
  58.9 14.0 %all_to_all.40 = f32[16,1,512]{2,1,0:T(1,128)S(1)} all-to-all(f32[16,1,512]{2,1,0:T(1,128)S(1)} %broadcast_in_dim.6), channel_id=1, replica_groups=mesh['outer'=16,'inner'=32] {'outer'}, dimensions={0} | all-to-all | bytes 65536 | tf_op jit(solution)/shard_map/all_to_all | solution.py:124
  72.8 1.1 broadcast_in_dim.15
  73.9 6.5 %all-to-all-start.3 = ((f32[32,16,512]{2,1,0:T(8,128)}), f32[32,16,512]{2,1,0:T(8,128)S(1)}, u32[]{:S(2)}, u32[]{:S(2)}) async-start(f32[32,16,512]{2,1,0:T(8,128)} %broadcast_in_dim.15), calls=%async_computation.3 | async-start | bytes 2097152 | tf_op jit(solution)/shard_map/all_to_all | solution.py:124
  80.5 0.0 copy-done.2
  80.5 1.7 %fusion.5.gram_ref = f32[256,256]{1,0:T(8,128)} fusion(f32[512,256]{1,0:T(8,128)S(1)} %copy-done.2), kind=kOutput, calls=%fused_computation.6 | convolution fusion | flops 402653184 | bytes 786432 | tf_op jit(solution)/shard_map/dot_general | solution.py:108
  82.2 17.2 %shard_map.41 = f32[512,256]{1,0:T(8,128)} custom-call(f32[256,256]{1,0:T(8,128)} %fusion.5.gram_ref, f32[512,256]{1,0:T(8,128)} %block_ref.1), custom_call_target="tpu_custom_call" | custom-call | tf_op jit(solution)/shard_map/pallas_call | solution.py:110
  99.4 0.0 all-to-all-done.3
  99.4 2.0 %fusion.6.block_ref = f32[512,256]{1,0:T(8,128)S(1)} fusion(f32[512,512]{1,0:T(8,128)S(1)} %bitcast.23, f32[512,256]{1,0:T(8,128)} %shard_map.41), kind=kOutput, calls=%fused_computation.7 | convolution fusion | flops 805306368 | bytes 2097152 | tf_op jit(solution)/shard_map/dot_general | solution.py:15
  101.4 0.0 copy-start.1
  101.4 1.7 %fusion.7.gram_ref = f32[256,256]{1,0:T(8,128)} fusion(f32[512,256]{1,0:T(8,128)S(1)} %fusion.6.block_ref), kind=kOutput, calls=%fused_computation.8 | convolution fusion | flops 402653184 | bytes 786432 | tf_op jit(solution)/shard_map/dot_general | solution.py:108
  103.2 0.0 copy-done.1
  103.2 17.4 %shard_map.42 = f32[512,256]{1,0:T(8,128)} custom-call(f32[256,256]{1,0:T(8,128)} %fusion.7.gram_ref, f32[512,256]{1,0:T(8,128)} %copy-done.1), custom_call_target="tpu_custom_call" | custom-call | tf_op jit(solution)/shard_map/pallas_call | solution.py:110
  120.5 2.0 %fusion.8.block_ref = f32[512,256]{1,0:T(8,128)S(1)} fusion(f32[512,512]{1,0:T(8,128)S(1)} %bitcast.24, f32[512,256]{1,0:T(8,128)} %shard_map.42), kind=kOutput, calls=%fused_computation.9 | convolution fusion | flops 805306368 | bytes 2097152 | tf_op jit(solution)/shard_map/dot_general | solution.py:15
  122.6 0.0 copy-start
  122.6 0.0 copy-start.3
  122.6 1.7 %fusion.9.gram_ref = f32[256,256]{1,0:T(8,128)} fusion(f32[512,256]{1,0:T(8,128)S(1)} %fusion.8.block_ref), kind=kOutput, calls=%fused_computation.10 | convolution fusion | flops 402653184 | bytes 786432 | tf_op jit(solution)/shard_map/dot_general | solution.py:108
  124.3 0.0 copy-done
  124.3 17.4 %shard_map.43 = f32[512,256]{1,0:T(8,128)} custom-call(f32[256,256]{1,0:T(8,128)} %fusion.9.gram_ref, f32[512,256]{1,0:T(8,128)} %copy-done), custom_call_target="tpu_custom_call" | custom-call | tf_op jit(solution)/shard_map/pallas_call | solution.py:110
  141.7 0.0 copy-done.3
  141.7 3.2 %fusion = f32[256,4,256]{2,0,1:T(8,128)S(1)} fusion(f32[512,4,256]{2,1,0:T(4,128)S(1)} %copy-done.3, f32[512,256]{1,0:T(8,128)} %shard_map.43), kind=kOutput, calls=%fused_computation | convolution fusion | flops 1610612736 | bytes 3670016 | tf_op jit(solution)/shard_map/dot_general | solution.py:144
  144.9 0.7 copy.13
  145.6 24.5 %all_to_all.41 = f32[256,4,256]{2,1,0:T(4,128)S(1)} all-to-all(f32[256,4,256]{2,1,0:T(4,128)S(1)} %copy.13), channel_id=1, replica_groups=mesh['outer'=16,'inner'=32] {'inner'}, dimensions={0} | all-to-all | bytes 2097152 | tf_op jit(solution)/shard_map/all_to_all | solution.py:148
  170.1 0.2 copy.14
  170.3 1.3 all_to_all.32
  (4 shorter events, 0.1 us)
Async XLA Ops:
  33.6 46.8 %copy-start.2 = (f32[512,256]{1,0:T(8,128)S(1)}, f32[512,256]{1,0:T(8,128)}, u32[]{:S(2)}) copy-start(f32[512,256]{1,0:T(8,128)} %block_ref.1) | copy-start | bytes 1572868
  73.9 25.5 %all-to-all-start.3 = ((f32[32,16,512]{2,1,0:T(8,128)}), f32[32,16,512]{2,1,0:T(8,128)S(1)}, u32[]{:S(2)}, u32[]{:S(2)}) async-start(f32[32,16,512]{2,1,0:T(8,128)} %broadcast_in_dim.15), calls=%async_computation.3 | async-start | bytes 2097152 | tf_op jit(solution)/shard_map/all_to_all | solution.py:124
  101.4 1.7 %copy-start.1 = (f32[512,256]{1,0:T(8,128)}, f32[512,256]{1,0:T(8,128)S(1)}, u32[]{:S(2)}) copy-start(f32[512,256]{1,0:T(8,128)S(1)} %fusion.6.block_ref) | copy-start | bytes 1572868
  122.6 1.7 %copy-start = (f32[512,256]{1,0:T(8,128)}, f32[512,256]{1,0:T(8,128)S(1)}, u32[]{:S(2)}) copy-start(f32[512,256]{1,0:T(8,128)S(1)} %fusion.8.block_ref) | copy-start | bytes 1572868
  122.6 19.2 %copy-start.3 = (f32[512,4,256]{2,1,0:T(4,128)S(1)}, f32[512,4,256]{2,1,0:T(4,128)}, u32[]{:S(2)}) copy-start(f32[512,4,256]{2,1,0:T(4,128)} %param.2) | copy-start | bytes 6291460

commit v5 on v4

--- a/solution.py
+++ b/solution.py
@@ -88,18 +88,22 @@
     eye_lane = lax.broadcasted_iota(jnp.int32, inv_ref.shape, 1)
     inv_ref[...] = jnp.where(eye_sub == eye_lane, 1.0, 0.0).astype(jnp.float32)
     rows = lax.broadcasted_iota(jnp.int32, (order, 1), 0)
-    pick_sub = lax.broadcasted_iota(jnp.int32, (wide, order), 0)
-    pick_lane = lax.broadcasted_iota(jnp.int32, (wide, order), 1)
-    for panel in range(order // PANEL):
+    lanes = lax.broadcasted_iota(jnp.int32, (order, wide), 1)
+    panels = order // PANEL
+    for panel in range(panels):
         low = panel * PANEL
-        pick = jnp.where((pick_lane == pick_sub + low) & (pick_sub < PANEL), 1.0, 0.0)
-        cols = mat_nt(rest_ref[...], pick.astype(jnp.float32))
+        base = low - low % wide
+        cols = rest_ref[:, base:base + wide]
+        if low % wide:
+            cols = pltpu.roll(cols, wide - low % wide, 1)
+        cols = jnp.where(lanes < PANEL, cols, 0.0)
         diag_inv = leaf_inverse_factor(cols[low:low + PANEL, :])
         factor = jnp.where(rows >= low, mat_nt(cols, diag_inv), 0.0)
-        rest_ref[...] = rest_ref[...] - mat_nt(factor, factor)
         solved = mat(diag_inv, inv_ref[low:low + wide, :])
-        below = jnp.where(rows >= low + PANEL, factor, 0.0)
-        inv_ref[0:order, :] = inv_ref[0:order, :] - mat(below, solved)
+        if panel + 1 < panels:
+            rest_ref[...] = rest_ref[...] - mat_nt(factor, factor)
+            below = jnp.where(rows >= low + PANEL, factor, 0.0)
+            inv_ref[0:order, :] = inv_ref[0:order, :] - mat(below, solved)
         inv_ref[low:low + PANEL, :] = solved
     out_ref[...] = mat_nt(block_ref[...], inv_ref[0:order, :])
 

time: 172 us -> 165 us (0.959)
  Pallas kernels: 52 us -> 44.7 us
    pallas_call x3, Pallas kernels: 52 us -> 44.7 us  [orthonormal(): pl.pallas_call(orth_kernel, out_shape=jax.ShapeDtypeStruct(block.shape, j...]
  transfers between devices with their start and end apart: 1 -> 1, of which waited for: 0 -> 1; matrix products, arithmetic and copies ran while one was open for 1% -> 1% of each run, Pallas kernels for 10% -> 9%
where the time goes in v5:
time: 165 us; the launch traced here: 164 us
  blocking collectives  89.6 us (54%)
  Pallas kernels  44.7 us (27%)
  matrix products  18.5 us (11%)
  starting transfers between devices  6.53 us (4%)
  local copies, waits for them, and re-layouts  3.37 us (2%)
    all_to_all x2, blocking collectives, scatter_sum(): return lax.all_to_all(pieces, axis_name, 0, 0, tiled=True).sum(0)  51.9 us
    pallas_call x3, Pallas kernels, orthonormal(): pl.pallas_call(orth_kernel, out_shape=jax.ShapeDtypeStruct(block.shape, j...  44.7 us
    all_to_all x1, blocking collectives, on_device(): lax.all_to_all(core_block, 'inner', split_axis=0, concat_axis=1, tiled=True)  23.8 us
    all_to_all x1, blocking collectives, gather_rows(): gathered = lax.all_to_all(copies, axis_name, 0, 0, tiled=True)  14 us
    all_to_all x1, starting transfers between devices, gather_rows(): gathered = lax.all_to_all(copies, axis_name, 0, 0, tiled=True)  6.53 us
    dot_general x1, matrix products, on_device(): lax.dot_general(field_slab, field_slab, (((1, 2), (1, 2)), ((), ())), pre...  6.13 us
    dot_general x3, matrix products, orthonormal(): jnp.dot(block.T, block, precision=lax.Precision.HIGHEST, preferred_elemen...  5.15 us
    dot_general x2, matrix products, product(): jnp.dot(first_mat, second_mat, precision=lax.Precision.HIGHEST, preferred...  4.05 us
  transfers between devices with their start and end apart: 1, of which 1 were waited for; matrix products, arithmetic and copies ran while one was open for 1% of the time, Pallas kernels for 9%

profile of v5, /device:TPU:1, one launch (start us, length us, event | category | flops | bytes accessed | tf_op | source)
XLA Modules:
  0.0 164.3 jit_solution(7992483984802158394)
XLA Ops:
  0.6 6.1 %fusion.2 = f32[512,512,1]{1,0,2:T(8,128)S(1)} fusion(f32[512,4,256]{2,1,0:T(4,128)} %param.2), kind=kOutput, calls=%fused_computation.2 | convolution fusion | flops 3221225472 | bytes 3145728 | tf_op jit(solution)/shard_map/dot_general | solution.py:140
  6.8 26.8 %all_to_all.38 = f32[32,16,512]{2,1,0:T(8,128)S(1)} all-to-all(f32[32,16,512]{2,1,0:T(8,128)S(1)} %bitcast.26), channel_id=1, replica_groups=mesh['outer'=16,'inner'=32] {'inner'}, dimensions={0} | all-to-all | bytes 2097152 | tf_op jit(solution)/shard_map/all_to_all | solution.py:123
  33.6 0.0 copy-start.2
  33.6 0.1 reduce_sum.18
  33.7 25.1 %all_to_all.39 = f32[16,1,512]{2,1,0:T(1,128)S(1)} all-to-all(f32[16,1,512]{2,1,0:T(1,128)S(1)} %reshape.20), channel_id=1, replica_groups=mesh['outer'=16,'inner'=32] {'outer'}, dimensions={0} | all-to-all | bytes 65536 | tf_op jit(solution)/shard_map/all_to_all | solution.py:123
  58.8 14.0 %all_to_all.40 = f32[16,1,512]{2,1,0:T(1,128)S(1)} all-to-all(f32[16,1,512]{2,1,0:T(1,128)S(1)} %broadcast_in_dim.6), channel_id=1, replica_groups=mesh['outer'=16,'inner'=32] {'outer'}, dimensions={0} | all-to-all | bytes 65536 | tf_op jit(solution)/shard_map/all_to_all | solution.py:128
  72.8 1.1 broadcast_in_dim.15
  73.9 6.5 %all-to-all-start.3 = ((f32[32,16,512]{2,1,0:T(8,128)}), f32[32,16,512]{2,1,0:T(8,128)S(1)}, u32[]{:S(2)}, u32[]{:S(2)}) async-start(f32[32,16,512]{2,1,0:T(8,128)} %broadcast_in_dim.15), calls=%async_computation.3 | async-start | bytes 2097152 | tf_op jit(solution)/shard_map/all_to_all | solution.py:128
  80.4 0.0 copy-done.2
  80.4 1.7 %fusion.5.gram_ref = f32[256,256]{1,0:T(8,128)} fusion(f32[512,256]{1,0:T(8,128)S(1)} %copy-done.2), kind=kOutput, calls=%fused_computation.6 | convolution fusion | flops 402653184 | bytes 786432 | tf_op jit(solution)/shard_map/dot_general | solution.py:112
  82.2 14.8 %shard_map.41 = f32[512,256]{1,0:T(8,128)} custom-call(f32[256,256]{1,0:T(8,128)} %fusion.5.gram_ref, f32[512,256]{1,0:T(8,128)} %block_ref.1), custom_call_target="tpu_custom_call" | custom-call | tf_op jit(solution)/shard_map/pallas_call | solution.py:114
  97.0 0.7 all-to-all-done.3
  97.7 2.0 %fusion.6.block_ref = f32[512,256]{1,0:T(8,128)S(1)} fusion(f32[512,512]{1,0:T(8,128)S(1)} %bitcast.23, f32[512,256]{1,0:T(8,128)} %shard_map.41), kind=kOutput, calls=%fused_computation.7 | convolution fusion | flops 805306368 | bytes 2097152 | tf_op jit(solution)/shard_map/dot_general | solution.py:15
  99.8 0.0 copy-start.1
  99.8 1.7 %fusion.7.gram_ref = f32[256,256]{1,0:T(8,128)} fusion(f32[512,256]{1,0:T(8,128)S(1)} %fusion.6.block_ref), kind=kOutput, calls=%fused_computation.8 | convolution fusion | flops 402653184 | bytes 786432 | tf_op jit(solution)/shard_map/dot_general | solution.py:112
  101.5 0.0 copy-done.1
  101.5 15.0 %shard_map.42 = f32[512,256]{1,0:T(8,128)} custom-call(f32[256,256]{1,0:T(8,128)} %fusion.7.gram_ref, f32[512,256]{1,0:T(8,128)} %copy-done.1), custom_call_target="tpu_custom_call" | custom-call | tf_op jit(solution)/shard_map/pallas_call | solution.py:114
  116.5 2.0 %fusion.8.block_ref = f32[512,256]{1,0:T(8,128)S(1)} fusion(f32[512,512]{1,0:T(8,128)S(1)} %bitcast.24, f32[512,256]{1,0:T(8,128)} %shard_map.42), kind=kOutput, calls=%fused_computation.9 | convolution fusion | flops 805306368 | bytes 2097152 | tf_op jit(solution)/shard_map/dot_general | solution.py:15
  118.5 0.0 copy-start
  118.5 0.0 copy-start.3
  118.6 1.7 %fusion.9.gram_ref = f32[256,256]{1,0:T(8,128)} fusion(f32[512,256]{1,0:T(8,128)S(1)} %fusion.8.block_ref), kind=kOutput, calls=%fused_computation.10 | convolution fusion | flops 402653184 | bytes 786432 | tf_op jit(solution)/shard_map/dot_general | solution.py:112
  120.3 0.0 copy-done
  120.3 14.8 %shard_map.43 = f32[512,256]{1,0:T(8,128)} custom-call(f32[256,256]{1,0:T(8,128)} %fusion.9.gram_ref, f32[512,256]{1,0:T(8,128)} %copy-done), custom_call_target="tpu_custom_call" | custom-call | tf_op jit(solution)/shard_map/pallas_call | solution.py:114
  135.1 0.0 copy-done.3
  135.1 3.2 %fusion = f32[256,4,256]{2,0,1:T(8,128)S(1)} fusion(f32[512,4,256]{2,1,0:T(4,128)S(1)} %copy-done.3, f32[512,256]{1,0:T(8,128)} %shard_map.43), kind=kOutput, calls=%fused_computation | convolution fusion | flops 1610612736 | bytes 3670016 | tf_op jit(solution)/shard_map/dot_general | solution.py:148
  138.3 0.7 copy.13
  139.0 23.8 %all_to_all.41 = f32[256,4,256]{2,1,0:T(4,128)S(1)} all-to-all(f32[256,4,256]{2,1,0:T(4,128)S(1)} %copy.13), channel_id=1, replica_groups=mesh['outer'=16,'inner'=32] {'inner'}, dimensions={0} | all-to-all | bytes 2097152 | tf_op jit(solution)/shard_map/all_to_all | solution.py:152
  162.8 0.2 copy.14
  163.0 1.3 all_to_all.32
  (4 shorter events, 0.1 us)
Async XLA Ops:
  33.6 46.8 %copy-start.2 = (f32[512,256]{1,0:T(8,128)S(1)}, f32[512,256]{1,0:T(8,128)}, u32[]{:S(2)}) copy-start(f32[512,256]{1,0:T(8,128)} %block_ref.1) | copy-start | bytes 1572868
  73.9 23.8 %all-to-all-start.3 = ((f32[32,16,512]{2,1,0:T(8,128)}), f32[32,16,512]{2,1,0:T(8,128)S(1)}, u32[]{:S(2)}, u32[]{:S(2)}) async-start(f32[32,16,512]{2,1,0:T(8,128)} %broadcast_in_dim.15), calls=%async_computation.3 | async-start | bytes 2097152 | tf_op jit(solution)/shard_map/all_to_all | solution.py:128
  99.8 1.7 %copy-start.1 = (f32[512,256]{1,0:T(8,128)}, f32[512,256]{1,0:T(8,128)S(1)}, u32[]{:S(2)}) copy-start(f32[512,256]{1,0:T(8,128)S(1)} %fusion.6.block_ref) | copy-start | bytes 1572868
  118.5 1.7 %copy-start = (f32[512,256]{1,0:T(8,128)}, f32[512,256]{1,0:T(8,128)S(1)}, u32[]{:S(2)}) copy-start(f32[512,256]{1,0:T(8,128)S(1)} %fusion.8.block_ref) | copy-start | bytes 1572868
  118.5 16.6 %copy-start.3 = (f32[512,4,256]{2,1,0:T(4,128)S(1)}, f32[512,4,256]{2,1,0:T(4,128)}, u32[]{:S(2)}) copy-start(f32[512,4,256]{2,1,0:T(4,128)} %param.2) | copy-start | bytes 6291460

commit v6 on v5

--- a/solution.py
+++ b/solution.py
@@ -80,10 +80,18 @@
     return jnp.where(lane < size, swapped, 0.0)
 
 
-def orth_kernel(gram_ref, block_ref, out_ref, rest_ref, inv_ref):
-    order = gram_ref.shape[0]
+def mat_tn(first, second):
+    return lax.dot_general(
+        first, second, (((0,), (0,)), ((), ())),
+        precision=lax.Precision.HIGHEST, preferred_element_type=jnp.float32,
+    )
+
+
+def factor_and_apply(block_ref, out_ref, rest_ref, inv_ref):
+    order = block_ref.shape[1]
     wide = 2 * PANEL
-    rest_ref[...] = gram_ref[...]
+    block = block_ref[...]
+    rest_ref[...] = mat_tn(block, block)
     eye_sub = lax.broadcasted_iota(jnp.int32, inv_ref.shape, 0)
     eye_lane = lax.broadcasted_iota(jnp.int32, inv_ref.shape, 1)
     inv_ref[...] = jnp.where(eye_sub == eye_lane, 1.0, 0.0).astype(jnp.float32)
@@ -108,14 +116,33 @@
     out_ref[...] = mat_nt(block_ref[...], inv_ref[0:order, :])
 
 
+def orth_kernel(block_ref, out_ref, rest_ref, inv_ref):
+    factor_and_apply(block_ref, out_ref, rest_ref, inv_ref)
+
+
+def power_orth_kernel(gram_ref, sub_ref, out_ref, rest_ref, inv_ref, block_ref):
+    block_ref[...] = mat(gram_ref[...], sub_ref[...])
+    factor_and_apply(block_ref, out_ref, rest_ref, inv_ref)
+
+
+def orth_scratch(order):
+    return [pltpu.VMEM((order, order), jnp.float32), pltpu.VMEM((order + PANEL, order), jnp.float32)]
+
+
 def orthonormal(block):
-    gram = jnp.dot(block.T, block, precision=lax.Precision.HIGHEST, preferred_element_type=jnp.float32)
-    order = block.shape[1]
     return pl.pallas_call(
         orth_kernel,
         out_shape=jax.ShapeDtypeStruct(block.shape, jnp.float32),
-        scratch_shapes=[pltpu.VMEM((order, order), jnp.float32), pltpu.VMEM((order + PANEL, order), jnp.float32)],
-    )(gram, block)
+        scratch_shapes=orth_scratch(block.shape[1]),
+    )(block)
+
+
+def power_orthonormal(gram, subspace):
+    return pl.pallas_call(
+        power_orth_kernel,
+        out_shape=jax.ShapeDtypeStruct(subspace.shape, jnp.float32),
+        scratch_shapes=orth_scratch(subspace.shape[1]) + [pltpu.VMEM(subspace.shape, jnp.float32)],
+    )(gram, subspace)
 
 
 def scatter_sum(block, axis_name, parts):
@@ -144,7 +171,7 @@
     subspace = orthonormal(start_block)
     gram_total = sum_everywhere(gram_local, sizes)
     for sweep_index in range(ITERS):
-        subspace = orthonormal(product(gram_total, subspace))
+        subspace = power_orthonormal(gram_total, subspace)
     core_block = lax.dot_general(
         subspace, field_slab, (((0,), (0,)), ((), ())),
         precision=lax.Precision.HIGHEST, preferred_element_type=jnp.float32,

time: 165 us -> 164 us (level)
  matrix products: 18.5 us -> 9.31 us
  Pallas kernels: 44.7 us -> 52.6 us
    pallas_call x0 -> x2, Pallas kernels: none -> 36.5 us  [power_orthonormal(): pl.pallas_call(power_orth_kernel, out_shape=jax.ShapeDtypeStruct(subspace...]
    pallas_call x3 -> x1, Pallas kernels: 44.7 us -> 16.1 us  [orthonormal(): pl.pallas_call(orth_kernel, out_shape=jax.ShapeDtypeStruct(block.shape, j...]
    dot_general x5 -> x0, matrix products: 9.2 us -> none  [the longest x3 5.15 us: orthonormal(): jnp.dot(block.T, block, precision=lax.Precision.HIGHEST, preferred_elemen...]
  transfers between devices with their start and end apart: 1 -> 1, of which waited for: 1 -> 1; matrix products, arithmetic and copies ran while one was open for 1% -> 0% of each run, Pallas kernels for 9% -> 10%
where the time goes in v6:
time: 164 us
  blocking collectives  89 us (54%)
  Pallas kernels  52.6 us (32%)
  matrix products  9.31 us (6%)
  starting transfers between devices  6.53 us (4%)
  local copies, waits for them, and re-layouts  4.32 us (3%)
    all_to_all x2, blocking collectives, scatter_sum(): return lax.all_to_all(pieces, axis_name, 0, 0, tiled=True).sum(0)  51.8 us
    pallas_call x2, Pallas kernels, power_orthonormal(): pl.pallas_call(power_orth_kernel, out_shape=jax.ShapeDtypeStruct(subspace...  36.5 us
    all_to_all x1, blocking collectives, on_device(): lax.all_to_all(core_block, 'inner', split_axis=0, concat_axis=1, tiled=True)  23.3 us
    pallas_call x1, Pallas kernels, orthonormal(): pl.pallas_call(orth_kernel, out_shape=jax.ShapeDtypeStruct(block.shape, j...  16.1 us
    all_to_all x1, blocking collectives, gather_rows(): gathered = lax.all_to_all(copies, axis_name, 0, 0, tiled=True)  14 us
    all_to_all x1, starting transfers between devices, gather_rows(): gathered = lax.all_to_all(copies, axis_name, 0, 0, tiled=True)  6.53 us
    dot_general x1, matrix products, on_device(): lax.dot_general(field_slab, field_slab, (((1, 2), (1, 2)), ((), ())), pre...  6.13 us
  transfers between devices with their start and end apart: 1, of which 1 were waited for; matrix products, arithmetic and copies ran while one was open for 0% of the time, Pallas kernels for 10%

profile of v6, /device:TPU:1, one launch (start us, length us, event | category | flops | bytes accessed | tf_op | source)
XLA Modules:
  0.0 163.7 jit_solution(4688422950171384121)
XLA Ops:
  0.6 6.1 %fusion.2 = f32[512,512,1]{1,0,2:T(8,128)S(1)} fusion(f32[512,4,256]{2,1,0:T(4,128)} %param.2), kind=kOutput, calls=%fused_computation.2 | convolution fusion | flops 3221225472 | bytes 3145728 | tf_op jit(solution)/shard_map/dot_general | solution.py:167
  6.8 26.8 %all_to_all.38 = f32[32,16,512]{2,1,0:T(8,128)S(1)} all-to-all(f32[32,16,512]{2,1,0:T(8,128)S(1)} %bitcast.16), channel_id=1, replica_groups=mesh['outer'=16,'inner'=32] {'inner'}, dimensions={0} | all-to-all | bytes 2097152 | tf_op jit(solution)/shard_map/all_to_all | solution.py:150
  33.6 0.1 reduce_sum.18
  33.7 24.9 %all_to_all.39 = f32[16,1,512]{2,1,0:T(1,128)S(1)} all-to-all(f32[16,1,512]{2,1,0:T(1,128)S(1)} %reshape.20), channel_id=1, replica_groups=mesh['outer'=16,'inner'=32] {'outer'}, dimensions={0} | all-to-all | bytes 65536 | tf_op jit(solution)/shard_map/all_to_all | solution.py:150
  58.7 14.0 %all_to_all.40 = f32[16,1,512]{2,1,0:T(1,128)S(1)} all-to-all(f32[16,1,512]{2,1,0:T(1,128)S(1)} %broadcast_in_dim.6), channel_id=1, replica_groups=mesh['outer'=16,'inner'=32] {'outer'}, dimensions={0} | all-to-all | bytes 65536 | tf_op jit(solution)/shard_map/all_to_all | solution.py:155
  72.7 1.1 broadcast_in_dim.15
  73.8 6.5 %all-to-all-start.3 = ((f32[32,16,512]{2,1,0:T(8,128)}), f32[32,16,512]{2,1,0:T(8,128)S(1)}, u32[]{:S(2)}, u32[]{:S(2)}) async-start(f32[32,16,512]{2,1,0:T(8,128)} %broadcast_in_dim.15), calls=%async_computation.3 | async-start | bytes 2097152 | tf_op jit(solution)/shard_map/all_to_all | solution.py:155
  80.3 16.1 %shard_map.41.sub_ref = f32[512,256]{1,0:T(8,128)} custom-call(f32[512,256]{1,0:T(8,128)} %block_ref.1), custom_call_target="tpu_custom_call" | custom-call | tf_op jit(solution)/shard_map/pallas_call | solution.py:133
  96.4 1.2 all-to-all-done.3
  97.6 0.0 copy-start
  97.6 1.0 copy-done
  98.6 0.0 copy-start.1
  98.6 18.4 %shard_map.42.sub_ref = f32[512,256]{1,0:T(8,128)} custom-call(f32[512,512]{1,0:T(8,128)} %bitcast.13, f32[512,256]{1,0:T(8,128)} %shard_map.41.sub_ref), custom_call_target="tpu_custom_call" | custom-call | tf_op jit(solution)/shard_map/pallas_call | solution.py:141
  117.0 18.1 %shard_map.43 = f32[512,256]{1,0:T(8,128)} custom-call(f32[512,512]{1,0:T(8,128)} %bitcast.14, f32[512,256]{1,0:T(8,128)} %shard_map.42.sub_ref), custom_call_target="tpu_custom_call" | custom-call | tf_op jit(solution)/shard_map/pallas_call | solution.py:141
  135.0 0.0 copy-done.1
  135.0 3.2 %fusion = f32[256,4,256]{2,0,1:T(8,128)S(1)} fusion(f32[512,4,256]{2,1,0:T(4,128)S(1)} %copy-done.1, f32[512,256]{1,0:T(8,128)} %shard_map.43), kind=kOutput, calls=%fused_computation | convolution fusion | flops 1610612736 | bytes 3670016 | tf_op jit(solution)/shard_map/dot_general | solution.py:175
  138.2 0.7 copy.13
  138.9 23.3 %all_to_all.41 = f32[256,4,256]{2,1,0:T(4,128)S(1)} all-to-all(f32[256,4,256]{2,1,0:T(4,128)S(1)} %copy.13), channel_id=1, replica_groups=mesh['outer'=16,'inner'=32] {'inner'}, dimensions={0} | all-to-all | bytes 2097152 | tf_op jit(solution)/shard_map/all_to_all | solution.py:179
  162.2 0.2 copy.14
  162.4 1.3 all_to_all.32
  (4 shorter events, 0.1 us)
Async XLA Ops:
  73.8 23.8 %all-to-all-start.3 = ((f32[32,16,512]{2,1,0:T(8,128)}), f32[32,16,512]{2,1,0:T(8,128)S(1)}, u32[]{:S(2)}, u32[]{:S(2)}) async-start(f32[32,16,512]{2,1,0:T(8,128)} %broadcast_in_dim.15), calls=%async_computation.3 | async-start | bytes 2097152 | tf_op jit(solution)/shard_map/all_to_all | solution.py:155
  97.6 1.0 copy-start
  98.6 36.5 %copy-start.1 = (f32[512,4,256]{2,1,0:T(4,128)S(1)}, f32[512,4,256]{2,1,0:T(4,128)}, u32[]{:S(2)}) copy-start(f32[512,4,256]{2,1,0:T(4,128)} %param.2) | copy-start | bytes 6291460

commit v7 on v6

--- a/solution.py
+++ b/solution.py
@@ -172,11 +172,17 @@
     gram_total = sum_everywhere(gram_local, sizes)
     for sweep_index in range(ITERS):
         subspace = power_orthonormal(gram_total, subspace)
+    ranks = subspace.shape[1]
+    parts = sizes["inner"]
     core_block = lax.dot_general(
         subspace, field_slab, (((0,), (0,)), ((), ())),
         precision=lax.Precision.HIGHEST, preferred_element_type=jnp.float32,
+    ).reshape(parts, ranks // parts, field_slab.shape[1] * field_slab.shape[2])
+    arrived = lax.all_to_all(core_block, "inner", 0, 0, tiled=True)
+    arrived = arrived.reshape(parts, ranks // parts, field_slab.shape[1], field_slab.shape[2])
+    core_fibres = jnp.transpose(arrived, (1, 0, 2, 3)).reshape(
+        ranks // parts, parts * field_slab.shape[1], field_slab.shape[2]
     )
-    core_fibres = lax.all_to_all(core_block, "inner", split_axis=0, concat_axis=1, tiled=True)
     return (subspace, core_fibres)
 
 

time: 164 us -> 165 us (level)
    reshape x0 -> x2, local copies, waits for them, and re-layouts: none -> 1.83 us  [the longest x1 1.29 us: on_device(): jnp.transpose(arrived, (1, 0, 2, 3))]
where the time goes in v7:
time: 165 us; the launch traced here: 164 us
  blocking collectives  89 us (54%)
  Pallas kernels  52.6 us (32%)
  matrix products  9.31 us (6%)
  starting transfers between devices  6.53 us (4%)
  local copies, waits for them, and re-layouts  4.63 us (3%)
    all_to_all x2, blocking collectives, scatter_sum(): return lax.all_to_all(pieces, axis_name, 0, 0, tiled=True).sum(0)  51.8 us
    pallas_call x2, Pallas kernels, power_orthonormal(): pl.pallas_call(power_orth_kernel, out_shape=jax.ShapeDtypeStruct(subspace...  36.5 us
    all_to_all x1, blocking collectives, on_device(): arrived = lax.all_to_all(core_block, 'inner', 0, 0, tiled=True)  23.3 us
    pallas_call x1, Pallas kernels, orthonormal(): pl.pallas_call(orth_kernel, out_shape=jax.ShapeDtypeStruct(block.shape, j...  16.1 us
    all_to_all x1, blocking collectives, gather_rows(): gathered = lax.all_to_all(copies, axis_name, 0, 0, tiled=True)  14 us
    all_to_all x1, starting transfers between devices, gather_rows(): gathered = lax.all_to_all(copies, axis_name, 0, 0, tiled=True)  6.53 us
    dot_general x1, matrix products, on_device(): lax.dot_general(field_slab, field_slab, (((1, 2), (1, 2)), ((), ())), pre...  6.13 us
  transfers between devices with their start and end apart: 1, of which 1 were waited for; matrix products, arithmetic and copies ran while one was open for 0% of the time, Pallas kernels for 10%

profile of v7, /device:TPU:1, one launch (start us, length us, event | category | flops | bytes accessed | tf_op | source)
XLA Modules:
  0.0 164.0 jit_solution(13783073933058558401)
XLA Ops:
  0.6 6.1 %fusion.2 = f32[512,512,1]{1,0,2:T(8,128)S(1)} fusion(f32[512,4,256]{2,1,0:T(4,128)} %param.2), kind=kOutput, calls=%fused_computation.2 | convolution fusion | flops 3221225472 | bytes 3145728 | tf_op jit(solution)/shard_map/dot_general | solution.py:167
  6.8 26.8 %all_to_all.25 = f32[32,16,512]{2,1,0:T(8,128)S(1)} all-to-all(f32[32,16,512]{2,1,0:T(8,128)S(1)} %bitcast.18), channel_id=1, replica_groups=mesh['outer'=16,'inner'=32] {'inner'}, dimensions={0} | all-to-all | bytes 2097152 | tf_op jit(solution)/shard_map/all_to_all | solution.py:150
  33.6 0.1 reduce_sum.18
  33.7 24.9 %all_to_all.26 = f32[16,1,512]{2,1,0:T(1,128)S(1)} all-to-all(f32[16,1,512]{2,1,0:T(1,128)S(1)} %reshape.29), channel_id=1, replica_groups=mesh['outer'=16,'inner'=32] {'outer'}, dimensions={0} | all-to-all | bytes 65536 | tf_op jit(solution)/shard_map/all_to_all | solution.py:150
  58.7 14.0 %all_to_all.27 = f32[16,1,512]{2,1,0:T(1,128)S(1)} all-to-all(f32[16,1,512]{2,1,0:T(1,128)S(1)} %broadcast_in_dim.6), channel_id=1, replica_groups=mesh['outer'=16,'inner'=32] {'outer'}, dimensions={0} | all-to-all | bytes 65536 | tf_op jit(solution)/shard_map/all_to_all | solution.py:155
  72.7 1.1 broadcast_in_dim.15
  73.8 6.5 %all-to-all-start.3 = ((f32[32,16,512]{2,1,0:T(8,128)}), f32[32,16,512]{2,1,0:T(8,128)S(1)}, u32[]{:S(2)}, u32[]{:S(2)}) async-start(f32[32,16,512]{2,1,0:T(8,128)} %broadcast_in_dim.15), calls=%async_computation.3 | async-start | bytes 2097152 | tf_op jit(solution)/shard_map/all_to_all | solution.py:155
  80.3 16.1 %shard_map.41.sub_ref = f32[512,256]{1,0:T(8,128)} custom-call(f32[512,256]{1,0:T(8,128)} %block_ref.1), custom_call_target="tpu_custom_call" | custom-call | tf_op jit(solution)/shard_map/pallas_call | solution.py:133
  96.4 1.2 all-to-all-done.3
  97.6 0.0 copy-start
  97.6 1.0 copy-done
  98.6 0.0 copy-start.1
  98.6 18.4 %shard_map.42.sub_ref = f32[512,256]{1,0:T(8,128)} custom-call(f32[512,512]{1,0:T(8,128)} %bitcast.15, f32[512,256]{1,0:T(8,128)} %shard_map.41.sub_ref), custom_call_target="tpu_custom_call" | custom-call | tf_op jit(solution)/shard_map/pallas_call | solution.py:141
  117.0 18.1 %shard_map.43 = f32[512,256]{1,0:T(8,128)} custom-call(f32[512,512]{1,0:T(8,128)} %bitcast.16, f32[512,256]{1,0:T(8,128)} %shard_map.42.sub_ref), custom_call_target="tpu_custom_call" | custom-call | tf_op jit(solution)/shard_map/pallas_call | solution.py:141
  135.0 0.0 copy-done.1
  135.0 3.2 %fusion = f32[256,4,256]{2,0,1:T(8,128)S(1)} fusion(f32[512,4,256]{2,1,0:T(4,128)S(1)} %copy-done.1, f32[512,256]{1,0:T(8,128)} %shard_map.43), kind=kOutput, calls=%fused_computation | convolution fusion | flops 1610612736 | bytes 3670016 | tf_op jit(solution)/shard_map/dot_general | solution.py:177
  138.2 0.7 copy.18
  138.9 0.5 reshape.31
  139.4 23.3 %all_to_all.28 = f32[32,8,1024]{2,1,0:T(8,128)S(1)} all-to-all(f32[32,8,1024]{2,1,0:T(8,128)S(1)} %reshape.31), channel_id=1, replica_groups=mesh['outer'=16,'inner'=32] {'inner'}, dimensions={0} | all-to-all | bytes 2097152 | tf_op jit(solution)/shard_map/all_to_all | solution.py:181
  162.7 1.3 copy.22
  (4 shorter events, 0.1 us)
Async XLA Ops:
  73.8 23.8 %all-to-all-start.3 = ((f32[32,16,512]{2,1,0:T(8,128)}), f32[32,16,512]{2,1,0:T(8,128)S(1)}, u32[]{:S(2)}, u32[]{:S(2)}) async-start(f32[32,16,512]{2,1,0:T(8,128)} %broadcast_in_dim.15), calls=%async_computation.3 | async-start | bytes 2097152 | tf_op jit(solution)/shard_map/all_to_all | solution.py:155
  97.6 1.0 copy-start
  98.6 36.5 %copy-start.1 = (f32[512,4,256]{2,1,0:T(4,128)S(1)}, f32[512,4,256]{2,1,0:T(4,128)}, u32[]{:S(2)}) copy-start(f32[512,4,256]{2,1,0:T(4,128)} %param.2) | copy-start | bytes 6291460

commit v8 on v6

--- a/solution.py
+++ b/solution.py
@@ -95,23 +95,26 @@
     eye_sub = lax.broadcasted_iota(jnp.int32, inv_ref.shape, 0)
     eye_lane = lax.broadcasted_iota(jnp.int32, inv_ref.shape, 1)
     inv_ref[...] = jnp.where(eye_sub == eye_lane, 1.0, 0.0).astype(jnp.float32)
-    rows = lax.broadcasted_iota(jnp.int32, (order, 1), 0)
-    lanes = lax.broadcasted_iota(jnp.int32, (order, wide), 1)
     panels = order // PANEL
     for panel in range(panels):
         low = panel * PANEL
+        ahead = low + PANEL
         base = low - low % wide
-        cols = rest_ref[:, base:base + wide]
+        cols = rest_ref[low:order, base:base + wide]
         if low % wide:
             cols = pltpu.roll(cols, wide - low % wide, 1)
+        lanes = lax.broadcasted_iota(jnp.int32, cols.shape, 1)
         cols = jnp.where(lanes < PANEL, cols, 0.0)
-        diag_inv = leaf_inverse_factor(cols[low:low + PANEL, :])
-        factor = jnp.where(rows >= low, mat_nt(cols, diag_inv), 0.0)
+        diag_inv = leaf_inverse_factor(cols[0:PANEL, :])
+        factor = mat_nt(cols, diag_inv)
         solved = mat(diag_inv, inv_ref[low:low + wide, :])
         if panel + 1 < panels:
-            rest_ref[...] = rest_ref[...] - mat_nt(factor, factor)
-            below = jnp.where(rows >= low + PANEL, factor, 0.0)
-            inv_ref[0:order, :] = inv_ref[0:order, :] - mat(below, solved)
+            tail = factor[PANEL:, :]
+            full = factor
+            if low:
+                full = jnp.concatenate([jnp.zeros((low, PANEL), jnp.float32), factor], axis=0)
+            rest_ref[ahead:order, :] = rest_ref[ahead:order, :] - mat_nt(tail, full)
+            inv_ref[ahead:order, :] = inv_ref[ahead:order, :] - mat(tail, solved)
         inv_ref[low:low + PANEL, :] = solved
     out_ref[...] = mat_nt(block_ref[...], inv_ref[0:order, :])
 

time: 164 us -> 162 us (0.988)
  Pallas kernels: 52.6 us -> 50 us
    pallas_call x2, Pallas kernels: 36.5 us -> 34.8 us  [power_orthonormal(): pl.pallas_call(power_orth_kernel, out_shape=jax.ShapeDtypeStruct(subspace...]
  transfers between devices with their start and end apart: 1 -> 1, of which waited for: 1 -> 1; matrix products, arithmetic and copies ran while one was open for 0% -> 0% of each run, Pallas kernels for 10% -> 9%
where the time goes in v8:
time: 162 us; the launch traced here: 161 us
  blocking collectives  88.2 us (54%)
  Pallas kernels  50 us (31%)
  matrix products  9.31 us (6%)
  starting transfers between devices  6.53 us (4%)
  local copies, waits for them, and re-layouts  4.32 us (3%)
  waiting for transfers between devices  2.03 us (1%)
    all_to_all x2, blocking collectives, scatter_sum(): return lax.all_to_all(pieces, axis_name, 0, 0, tiled=True).sum(0)  51.8 us
    pallas_call x2, Pallas kernels, power_orthonormal(): pl.pallas_call(power_orth_kernel, out_shape=jax.ShapeDtypeStruct(subspace...  34.8 us
    all_to_all x1, blocking collectives, on_device(): lax.all_to_all(core_block, 'inner', split_axis=0, concat_axis=1, tiled=True)  22.4 us
    pallas_call x1, Pallas kernels, orthonormal(): pl.pallas_call(orth_kernel, out_shape=jax.ShapeDtypeStruct(block.shape, j...  15.2 us
    all_to_all x1, blocking collectives, gather_rows(): gathered = lax.all_to_all(copies, axis_name, 0, 0, tiled=True)  14 us
    all_to_all x1, starting transfers between devices, gather_rows(): gathered = lax.all_to_all(copies, axis_name, 0, 0, tiled=True)  6.53 us
    dot_general x1, matrix products, on_device(): lax.dot_general(field_slab, field_slab, (((1, 2), (1, 2)), ((), ())), pre...  6.13 us
  transfers between devices with their start and end apart: 1, of which 1 were waited for; matrix products, arithmetic and copies ran while one was open for 0% of the time, Pallas kernels for 9%

profile of v8, /device:TPU:1, one launch (start us, length us, event | category | flops | bytes accessed | tf_op | source)
XLA Modules:
  0.0 161.1 jit_solution(17550875170358856055)
XLA Ops:
  0.6 6.1 %fusion.2 = f32[512,512,1]{1,0,2:T(8,128)S(1)} fusion(f32[512,4,256]{2,1,0:T(4,128)} %param.2), kind=kOutput, calls=%fused_computation.2 | convolution fusion | flops 3221225472 | bytes 3145728 | tf_op jit(solution)/shard_map/dot_general | solution.py:170
  6.8 26.8 %all_to_all.38 = f32[32,16,512]{2,1,0:T(8,128)S(1)} all-to-all(f32[32,16,512]{2,1,0:T(8,128)S(1)} %bitcast.16), channel_id=1, replica_groups=mesh['outer'=16,'inner'=32] {'inner'}, dimensions={0} | all-to-all | bytes 2097152 | tf_op jit(solution)/shard_map/all_to_all | solution.py:153
  33.6 0.1 reduce_sum.18
  33.7 24.9 %all_to_all.39 = f32[16,1,512]{2,1,0:T(1,128)S(1)} all-to-all(f32[16,1,512]{2,1,0:T(1,128)S(1)} %reshape.20), channel_id=1, replica_groups=mesh['outer'=16,'inner'=32] {'outer'}, dimensions={0} | all-to-all | bytes 65536 | tf_op jit(solution)/shard_map/all_to_all | solution.py:153
  58.7 14.0 %all_to_all.40 = f32[16,1,512]{2,1,0:T(1,128)S(1)} all-to-all(f32[16,1,512]{2,1,0:T(1,128)S(1)} %broadcast_in_dim.6), channel_id=1, replica_groups=mesh['outer'=16,'inner'=32] {'outer'}, dimensions={0} | all-to-all | bytes 65536 | tf_op jit(solution)/shard_map/all_to_all | solution.py:158
  72.7 1.1 broadcast_in_dim.15
  73.8 6.5 %all-to-all-start.3 = ((f32[32,16,512]{2,1,0:T(8,128)}), f32[32,16,512]{2,1,0:T(8,128)S(1)}, u32[]{:S(2)}, u32[]{:S(2)}) async-start(f32[32,16,512]{2,1,0:T(8,128)} %broadcast_in_dim.15), calls=%async_computation.3 | async-start | bytes 2097152 | tf_op jit(solution)/shard_map/all_to_all | solution.py:158
  80.3 15.2 %shard_map.41.sub_ref = f32[512,256]{1,0:T(8,128)} custom-call(f32[512,256]{1,0:T(8,128)} %block_ref.1), custom_call_target="tpu_custom_call" | custom-call | tf_op jit(solution)/shard_map/pallas_call | solution.py:136
  95.6 2.0 %all-to-all-done.3 = f32[32,16,512]{2,1,0:T(8,128)S(1)} async-done(((f32[32,16,512]{2,1,0:T(8,128)}), f32[32,16,512]{2,1,0:T(8,128)S(1)}, u32[]{:S(2)}, u32[]{:S(2)}) %all-to-all-start.3) | async-done | bytes 1048608 | tf_op jit(solution)/shard_map/all_to_all | solution.py:158
  97.6 0.0 copy-start
  97.6 1.0 copy-done
  98.6 0.0 copy-start.1
  98.6 17.4 %shard_map.42.sub_ref = f32[512,256]{1,0:T(8,128)} custom-call(f32[512,512]{1,0:T(8,128)} %bitcast.13, f32[512,256]{1,0:T(8,128)} %shard_map.41.sub_ref), custom_call_target="tpu_custom_call" | custom-call | tf_op jit(solution)/shard_map/pallas_call | solution.py:144
  115.9 17.4 %shard_map.43 = f32[512,256]{1,0:T(8,128)} custom-call(f32[512,512]{1,0:T(8,128)} %bitcast.14, f32[512,256]{1,0:T(8,128)} %shard_map.42.sub_ref), custom_call_target="tpu_custom_call" | custom-call | tf_op jit(solution)/shard_map/pallas_call | solution.py:144
  133.3 0.0 copy-done.1
  133.3 3.2 %fusion = f32[256,4,256]{2,0,1:T(8,128)S(1)} fusion(f32[512,4,256]{2,1,0:T(4,128)S(1)} %copy-done.1, f32[512,256]{1,0:T(8,128)} %shard_map.43), kind=kOutput, calls=%fused_computation | convolution fusion | flops 1610612736 | bytes 3670016 | tf_op jit(solution)/shard_map/dot_general | solution.py:178
  136.5 0.7 copy.13
  137.2 22.4 %all_to_all.41 = f32[256,4,256]{2,1,0:T(4,128)S(1)} all-to-all(f32[256,4,256]{2,1,0:T(4,128)S(1)} %copy.13), channel_id=1, replica_groups=mesh['outer'=16,'inner'=32] {'inner'}, dimensions={0} | all-to-all | bytes 2097152 | tf_op jit(solution)/shard_map/all_to_all | solution.py:182
  159.6 0.2 copy.14
  159.8 1.3 all_to_all.32
  (4 shorter events, 0.1 us)
Async XLA Ops:
  73.8 23.8 %all-to-all-start.3 = ((f32[32,16,512]{2,1,0:T(8,128)}), f32[32,16,512]{2,1,0:T(8,128)S(1)}, u32[]{:S(2)}, u32[]{:S(2)}) async-start(f32[32,16,512]{2,1,0:T(8,128)} %broadcast_in_dim.15), calls=%async_computation.3 | async-start | bytes 2097152 | tf_op jit(solution)/shard_map/all_to_all | solution.py:158
  97.6 1.0 copy-start
  98.6 34.8 %copy-start.1 = (f32[512,4,256]{2,1,0:T(4,128)S(1)}, f32[512,4,256]{2,1,0:T(4,128)}, u32[]{:S(2)}) copy-start(f32[512,4,256]{2,1,0:T(4,128)} %param.2) | copy-start | bytes 6291460

commit v9 on v8

--- a/solution.py
+++ b/solution.py
@@ -107,15 +107,16 @@
         cols = jnp.where(lanes < PANEL, cols, 0.0)
         diag_inv = leaf_inverse_factor(cols[0:PANEL, :])
         factor = mat_nt(cols, diag_inv)
-        solved = mat(diag_inv, inv_ref[low:low + wide, :])
+        span = -(-ahead // wide) * wide
+        solved = mat(diag_inv, inv_ref[low:low + wide, 0:span])
         if panel + 1 < panels:
             tail = factor[PANEL:, :]
             full = factor
             if low:
                 full = jnp.concatenate([jnp.zeros((low, PANEL), jnp.float32), factor], axis=0)
-            rest_ref[ahead:order, :] = rest_ref[ahead:order, :] - mat_nt(tail, full)
-            inv_ref[ahead:order, :] = inv_ref[ahead:order, :] - mat(tail, solved)
-        inv_ref[low:low + PANEL, :] = solved
+            rest_ref[ahead:order, base:order] = rest_ref[ahead:order, base:order] - mat_nt(tail, full[base:, :])
+            inv_ref[ahead:order, 0:span] = inv_ref[ahead:order, 0:span] - mat(tail, solved)
+        inv_ref[low:low + PANEL, 0:span] = solved
     out_ref[...] = mat_nt(block_ref[...], inv_ref[0:order, :])
 
 

time: 162 us -> 161 us (level)
  no operation moved by 1% of the time
where the time goes in v9:
time: 161 us
  blocking collectives  88 us (55%)
  Pallas kernels  49.6 us (31%)
  matrix products  9.31 us (6%)
  starting transfers between devices  6.53 us (4%)
  local copies, waits for them, and re-layouts  4.32 us (3%)
  waiting for transfers between devices  2.18 us (1%)
    all_to_all x2, blocking collectives, scatter_sum(): return lax.all_to_all(pieces, axis_name, 0, 0, tiled=True).sum(0)  51.8 us
    pallas_call x2, Pallas kernels, power_orthonormal(): pl.pallas_call(power_orth_kernel, out_shape=jax.ShapeDtypeStruct(subspace...  34.5 us
    all_to_all x1, blocking collectives, on_device(): lax.all_to_all(core_block, 'inner', split_axis=0, concat_axis=1, tiled=True)  22.3 us
    pallas_call x1, Pallas kernels, orthonormal(): pl.pallas_call(orth_kernel, out_shape=jax.ShapeDtypeStruct(block.shape, j...  15.1 us
    all_to_all x1, blocking collectives, gather_rows(): gathered = lax.all_to_all(copies, axis_name, 0, 0, tiled=True)  14 us
    all_to_all x1, starting transfers between devices, gather_rows(): gathered = lax.all_to_all(copies, axis_name, 0, 0, tiled=True)  6.53 us
    dot_general x1, matrix products, on_device(): lax.dot_general(field_slab, field_slab, (((1, 2), (1, 2)), ((), ())), pre...  6.13 us
  transfers between devices with their start and end apart: 1, of which 1 were waited for; matrix products, arithmetic and copies ran while one was open for 0% of the time, Pallas kernels for 9%

profile of v9, /device:TPU:1, one launch (start us, length us, event | category | flops | bytes accessed | tf_op | source)
XLA Modules:
  0.0 160.8 jit_solution(3451855225419110632)
XLA Ops:
  0.6 6.1 %fusion.2 = f32[512,512,1]{1,0,2:T(8,128)S(1)} fusion(f32[512,4,256]{2,1,0:T(4,128)} %param.2), kind=kOutput, calls=%fused_computation.2 | convolution fusion | flops 3221225472 | bytes 3145728 | tf_op jit(solution)/shard_map/dot_general | solution.py:171
  6.8 26.8 %all_to_all.38 = f32[32,16,512]{2,1,0:T(8,128)S(1)} all-to-all(f32[32,16,512]{2,1,0:T(8,128)S(1)} %bitcast.16), channel_id=1, replica_groups=mesh['outer'=16,'inner'=32] {'inner'}, dimensions={0} | all-to-all | bytes 2097152 | tf_op jit(solution)/shard_map/all_to_all | solution.py:154
  33.6 0.1 reduce_sum.18
  33.7 24.9 %all_to_all.39 = f32[16,1,512]{2,1,0:T(1,128)S(1)} all-to-all(f32[16,1,512]{2,1,0:T(1,128)S(1)} %reshape.20), channel_id=1, replica_groups=mesh['outer'=16,'inner'=32] {'outer'}, dimensions={0} | all-to-all | bytes 65536 | tf_op jit(solution)/shard_map/all_to_all | solution.py:154
  58.7 14.0 %all_to_all.40 = f32[16,1,512]{2,1,0:T(1,128)S(1)} all-to-all(f32[16,1,512]{2,1,0:T(1,128)S(1)} %broadcast_in_dim.6), channel_id=1, replica_groups=mesh['outer'=16,'inner'=32] {'outer'}, dimensions={0} | all-to-all | bytes 65536 | tf_op jit(solution)/shard_map/all_to_all | solution.py:159
  72.7 1.1 broadcast_in_dim.15
  73.8 6.5 %all-to-all-start.3 = ((f32[32,16,512]{2,1,0:T(8,128)}), f32[32,16,512]{2,1,0:T(8,128)S(1)}, u32[]{:S(2)}, u32[]{:S(2)}) async-start(f32[32,16,512]{2,1,0:T(8,128)} %broadcast_in_dim.15), calls=%async_computation.3 | async-start | bytes 2097152 | tf_op jit(solution)/shard_map/all_to_all | solution.py:159
  80.3 15.1 %shard_map.41.sub_ref = f32[512,256]{1,0:T(8,128)} custom-call(f32[512,256]{1,0:T(8,128)} %block_ref.1), custom_call_target="tpu_custom_call" | custom-call | tf_op jit(solution)/shard_map/pallas_call | solution.py:137
  95.4 2.2 %all-to-all-done.3 = f32[32,16,512]{2,1,0:T(8,128)S(1)} async-done(((f32[32,16,512]{2,1,0:T(8,128)}), f32[32,16,512]{2,1,0:T(8,128)S(1)}, u32[]{:S(2)}, u32[]{:S(2)}) %all-to-all-start.3) | async-done | bytes 1048608 | tf_op jit(solution)/shard_map/all_to_all | solution.py:159
  97.6 0.0 copy-start
  97.6 1.0 copy-done
  98.6 0.0 copy-start.1
  98.6 17.2 %shard_map.42.sub_ref = f32[512,256]{1,0:T(8,128)} custom-call(f32[512,512]{1,0:T(8,128)} %bitcast.13, f32[512,256]{1,0:T(8,128)} %shard_map.41.sub_ref), custom_call_target="tpu_custom_call" | custom-call | tf_op jit(solution)/shard_map/pallas_call | solution.py:145
  115.8 17.3 %shard_map.43 = f32[512,256]{1,0:T(8,128)} custom-call(f32[512,512]{1,0:T(8,128)} %bitcast.14, f32[512,256]{1,0:T(8,128)} %shard_map.42.sub_ref), custom_call_target="tpu_custom_call" | custom-call | tf_op jit(solution)/shard_map/pallas_call | solution.py:145
  133.1 0.0 copy-done.1
  133.1 3.2 %fusion = f32[256,4,256]{2,0,1:T(8,128)S(1)} fusion(f32[512,4,256]{2,1,0:T(4,128)S(1)} %copy-done.1, f32[512,256]{1,0:T(8,128)} %shard_map.43), kind=kOutput, calls=%fused_computation | convolution fusion | flops 1610612736 | bytes 3670016 | tf_op jit(solution)/shard_map/dot_general | solution.py:179
  136.3 0.7 copy.13
  136.9 22.3 %all_to_all.41 = f32[256,4,256]{2,1,0:T(4,128)S(1)} all-to-all(f32[256,4,256]{2,1,0:T(4,128)S(1)} %copy.13), channel_id=1, replica_groups=mesh['outer'=16,'inner'=32] {'inner'}, dimensions={0} | all-to-all | bytes 2097152 | tf_op jit(solution)/shard_map/all_to_all | solution.py:183
  159.2 0.2 copy.14
  159.4 1.3 all_to_all.32
  (4 shorter events, 0.1 us)
Async XLA Ops:
  73.8 23.8 %all-to-all-start.3 = ((f32[32,16,512]{2,1,0:T(8,128)}), f32[32,16,512]{2,1,0:T(8,128)S(1)}, u32[]{:S(2)}, u32[]{:S(2)}) async-start(f32[32,16,512]{2,1,0:T(8,128)} %broadcast_in_dim.15), calls=%async_computation.3 | async-start | bytes 2097152 | tf_op jit(solution)/shard_map/all_to_all | solution.py:159
  97.6 1.0 copy-start
  98.6 34.5 %copy-start.1 = (f32[512,4,256]{2,1,0:T(4,128)S(1)}, f32[512,4,256]{2,1,0:T(4,128)}, u32[]{:S(2)}) copy-start(f32[512,4,256]{2,1,0:T(4,128)} %param.2) | copy-start | bytes 6291460

commit v10 on v8

--- a/solution.py
+++ b/solution.py
@@ -107,7 +107,10 @@
         cols = jnp.where(lanes < PANEL, cols, 0.0)
         diag_inv = leaf_inverse_factor(cols[0:PANEL, :])
         factor = mat_nt(cols, diag_inv)
-        solved = mat(diag_inv, inv_ref[low:low + wide, :])
+        if low:
+            solved = mat(diag_inv, inv_ref[low:low + wide, :])
+        else:
+            solved = jnp.concatenate([diag_inv, jnp.zeros((PANEL, order - wide), jnp.float32)], axis=1)
         if panel + 1 < panels:
             tail = factor[PANEL:, :]
             full = factor

time: 162 us -> 161 us (level)
  no operation moved by 1% of the time
where the time goes in v10:
time: 161 us
  blocking collectives  88.1 us (55%)
  Pallas kernels  49.7 us (31%)
  matrix products  9.31 us (6%)
  starting transfers between devices  6.53 us (4%)
  local copies, waits for them, and re-layouts  4.32 us (3%)
  waiting for transfers between devices  2.09 us (1%)
    all_to_all x2, blocking collectives, scatter_sum(): return lax.all_to_all(pieces, axis_name, 0, 0, tiled=True).sum(0)  51.8 us
    pallas_call x2, Pallas kernels, power_orthonormal(): pl.pallas_call(power_orth_kernel, out_shape=jax.ShapeDtypeStruct(subspace...  34.5 us
    all_to_all x1, blocking collectives, on_device(): lax.all_to_all(core_block, 'inner', split_axis=0, concat_axis=1, tiled=True)  22.4 us
    pallas_call x1, Pallas kernels, orthonormal(): pl.pallas_call(orth_kernel, out_shape=jax.ShapeDtypeStruct(block.shape, j...  15.2 us
    all_to_all x1, blocking collectives, gather_rows(): gathered = lax.all_to_all(copies, axis_name, 0, 0, tiled=True)  14 us
    all_to_all x1, starting transfers between devices, gather_rows(): gathered = lax.all_to_all(copies, axis_name, 0, 0, tiled=True)  6.53 us
    dot_general x1, matrix products, on_device(): lax.dot_general(field_slab, field_slab, (((1, 2), (1, 2)), ((), ())), pre...  6.13 us
  transfers between devices with their start and end apart: 1, of which 1 were waited for; matrix products, arithmetic and copies ran while one was open for 0% of the time, Pallas kernels for 9%

profile of v10, /device:TPU:1, one launch (start us, length us, event | category | flops | bytes accessed | tf_op | source)
XLA Modules:
  0.0 160.9 jit_solution(8274383440860601844)
XLA Ops:
  0.6 6.1 %fusion.2 = f32[512,512,1]{1,0,2:T(8,128)S(1)} fusion(f32[512,4,256]{2,1,0:T(4,128)} %param.2), kind=kOutput, calls=%fused_computation.2 | convolution fusion | flops 3221225472 | bytes 3145728 | tf_op jit(solution)/shard_map/dot_general | solution.py:173
  6.8 26.8 %all_to_all.38 = f32[32,16,512]{2,1,0:T(8,128)S(1)} all-to-all(f32[32,16,512]{2,1,0:T(8,128)S(1)} %bitcast.16), channel_id=1, replica_groups=mesh['outer'=16,'inner'=32] {'inner'}, dimensions={0} | all-to-all | bytes 2097152 | tf_op jit(solution)/shard_map/all_to_all | solution.py:156
  33.6 0.1 reduce_sum.18
  33.7 24.9 %all_to_all.39 = f32[16,1,512]{2,1,0:T(1,128)S(1)} all-to-all(f32[16,1,512]{2,1,0:T(1,128)S(1)} %reshape.20), channel_id=1, replica_groups=mesh['outer'=16,'inner'=32] {'outer'}, dimensions={0} | all-to-all | bytes 65536 | tf_op jit(solution)/shard_map/all_to_all | solution.py:156
  58.7 14.0 %all_to_all.40 = f32[16,1,512]{2,1,0:T(1,128)S(1)} all-to-all(f32[16,1,512]{2,1,0:T(1,128)S(1)} %broadcast_in_dim.6), channel_id=1, replica_groups=mesh['outer'=16,'inner'=32] {'outer'}, dimensions={0} | all-to-all | bytes 65536 | tf_op jit(solution)/shard_map/all_to_all | solution.py:161
  72.7 1.1 broadcast_in_dim.15
  73.8 6.5 %all-to-all-start.3 = ((f32[32,16,512]{2,1,0:T(8,128)}), f32[32,16,512]{2,1,0:T(8,128)S(1)}, u32[]{:S(2)}, u32[]{:S(2)}) async-start(f32[32,16,512]{2,1,0:T(8,128)} %broadcast_in_dim.15), calls=%async_computation.3 | async-start | bytes 2097152 | tf_op jit(solution)/shard_map/all_to_all | solution.py:161
  80.3 15.2 %shard_map.41.sub_ref = f32[512,256]{1,0:T(8,128)} custom-call(f32[512,256]{1,0:T(8,128)} %block_ref.1), custom_call_target="tpu_custom_call" | custom-call | tf_op jit(solution)/shard_map/pallas_call | solution.py:139
  95.5 2.1 %all-to-all-done.3 = f32[32,16,512]{2,1,0:T(8,128)S(1)} async-done(((f32[32,16,512]{2,1,0:T(8,128)}), f32[32,16,512]{2,1,0:T(8,128)S(1)}, u32[]{:S(2)}, u32[]{:S(2)}) %all-to-all-start.3) | async-done | bytes 1048608 | tf_op jit(solution)/shard_map/all_to_all | solution.py:161
  97.6 0.0 copy-start
  97.6 1.0 copy-done
  98.6 0.0 copy-start.1
  98.6 17.3 %shard_map.42.sub_ref = f32[512,256]{1,0:T(8,128)} custom-call(f32[512,512]{1,0:T(8,128)} %bitcast.13, f32[512,256]{1,0:T(8,128)} %shard_map.41.sub_ref), custom_call_target="tpu_custom_call" | custom-call | tf_op jit(solution)/shard_map/pallas_call | solution.py:147
  115.8 17.3 %shard_map.43 = f32[512,256]{1,0:T(8,128)} custom-call(f32[512,512]{1,0:T(8,128)} %bitcast.14, f32[512,256]{1,0:T(8,128)} %shard_map.42.sub_ref), custom_call_target="tpu_custom_call" | custom-call | tf_op jit(solution)/shard_map/pallas_call | solution.py:147
  133.1 0.0 copy-done.1
  133.1 3.2 %fusion = f32[256,4,256]{2,0,1:T(8,128)S(1)} fusion(f32[512,4,256]{2,1,0:T(4,128)S(1)} %copy-done.1, f32[512,256]{1,0:T(8,128)} %shard_map.43), kind=kOutput, calls=%fused_computation | convolution fusion | flops 1610612736 | bytes 3670016 | tf_op jit(solution)/shard_map/dot_general | solution.py:181
  136.3 0.7 copy.13
  137.0 22.4 %all_to_all.41 = f32[256,4,256]{2,1,0:T(4,128)S(1)} all-to-all(f32[256,4,256]{2,1,0:T(4,128)S(1)} %copy.13), channel_id=1, replica_groups=mesh['outer'=16,'inner'=32] {'inner'}, dimensions={0} | all-to-all | bytes 2097152 | tf_op jit(solution)/shard_map/all_to_all | solution.py:185
  159.4 0.2 copy.14
  159.6 1.3 all_to_all.32
  (4 shorter events, 0.1 us)
Async XLA Ops:
  73.8 23.8 %all-to-all-start.3 = ((f32[32,16,512]{2,1,0:T(8,128)}), f32[32,16,512]{2,1,0:T(8,128)S(1)}, u32[]{:S(2)}, u32[]{:S(2)}) async-start(f32[32,16,512]{2,1,0:T(8,128)} %broadcast_in_dim.15), calls=%async_computation.3 | async-start | bytes 2097152 | tf_op jit(solution)/shard_map/all_to_all | solution.py:161
  97.6 1.0 copy-start
  98.6 34.6 %copy-start.1 = (f32[512,4,256]{2,1,0:T(4,128)S(1)}, f32[512,4,256]{2,1,0:T(4,128)}, u32[]{:S(2)}) copy-start(f32[512,4,256]{2,1,0:T(4,128)} %param.2) | copy-start | bytes 6291460
